TPU v7x, 128 devices: a whole 4x4x4 slice. The times are simulated.
128 devices in a mesh: tod: 16 (over z, x), map: 8 (over y, core).
Axes of the slice: x: 4, y: 4, z: 4, core: 2. Of those that a mesh axis runs over, the one named last changes fastest.
Arguments:
- tod: float32 [128, 65536], P('map', 'tod'), may hold values from -6 to 6
- det_angle: float32 [128], P('map'), may hold values from -3.140625 to 3.140625
- angle_index: int32 [128, 65536], P('map', 'tod'), may hold values from 0 to 63
- offsets: int32 [128, 65536], P('map', 'tod'), may hold values from 0 to 255
- block_slot: int32 [128, 256], P('map', 'tod'), may hold values from 0 to 255, as said below
- hit_tiles: int32 [128, 128, 2], P(('tod', 'map')), may hold values from -1 to 383, as said below
- noise_filter: float32 [128, 129], P('map'), may hold values from -0.9 to 2, as said below
- precond: float32 [49152, 6, 256], P(('tod', 'map')), may hold values from -0.45 to 1, as said below
Outputs:
- solution: float32 [49152, 3, 256], P(('tod', 'map'))
- residual: float32 [49152, 3, 256], P(('tod', 'map'))
Inputs may be any that keep to these rules, and one draw needn't show every extreme that they name: `hit_tiles`: entry [g, o, j] is slot j of owner o's tiles touched by shard g, a tile index within the owner's 384 tiles, or -1 for an empty slot; used slots come first in a row and hold distinct tiles; some owner has all 2 slots used from every shard. `block_slot`: each entry h names a used slot, hit_tiles[g, h // 2, h % 2] >= 0, of the shard g that holds the block. `noise_filter`: each row defines a symmetric positive definite Toeplitz filter. `precond`: each pixel's 3x3 block is symmetric positive definite.
All inputs are finite; a program needn't handle non-finite values.
Results may differ from a plain program's by a relative error of at most 0.00028.
Values sent between devices are 32-bit elements; how exact they have to be, the bound alone decides.
No kernel may reach another device: no remote copies, remote signals or barrier semaphores. Data moves between devices by JAX's collectives and lax.ppermute only.
A program may use at most 64 MiB of HBM per device.

v0:
```python
import functools

import jax
import jax.numpy as jnp
from jax import lax
from jax.experimental import pallas as pl
from jax.experimental.pallas import tpu as pltpu
from jax.sharding import PartitionSpec as P

ANGLES = 64
ITERS = 2
SIDE = 128


def extended(cells, sides, width):
    for axis, dim in sides:
        count = lax.axis_size(axis)
        ends = count - 1
        head = lax.slice_in_dim(cells, 0, width, axis=dim)
        tail = lax.slice_in_dim(cells, cells.shape[dim] - width, cells.shape[dim], axis=dim)
        cells = jnp.concatenate(
            [
                lax.ppermute(tail, axis, [(i, (i + 1) % count) for i in range(ends)]),
                cells,
                lax.ppermute(head, axis, [((i + 1) % count, i) for i in range(ends)]),
            ],
            axis=dim,
        )
    return cells


def precondition(field, precond):
    tile = precond.shape[2]
    first, second, third = (field[:, 0:tile], field[:, tile : 2 * tile], field[:, 2 * tile :])
    row_one = precond[:, 0] * first + precond[:, 3] * second + precond[:, 4] * third
    row_two = precond[:, 3] * first + precond[:, 1] * second + precond[:, 5] * third
    row_three = precond[:, 4] * first + precond[:, 5] * second + precond[:, 2] * third
    return jnp.concatenate([row_one, row_two, row_three], axis=1)


def exchange(rows, partial, lists=None):
    shards = rows.shape[0]
    lane = jnp.arange(SIDE, dtype=jnp.int32)[None, :]
    extra = jnp.zeros((shards, SIDE), jnp.float32)
    if partial is not None:
        extra = jnp.where(lane == 0, partial.astype(jnp.float32), extra)
    if lists is not None:
        for k in range(lists.shape[1]):
            extra = jnp.where(lane == 1 + k, lists[:, k : k + 1].astype(jnp.float32), extra)
    rows = jnp.concatenate([rows, extra], axis=1)
    got = lax.all_to_all(rows, ("tod", "map"), split_axis=0, concat_axis=0, tiled=True)
    width = got.shape[1] - SIDE
    total = jnp.sum(got[:, width])
    if lists is None:
        return got[:, :width], total
    arrived_lists = jnp.round(got[:, width + 1 : width + 1 + lists.shape[1]]).astype(jnp.int32)
    return got[:, :width], total, arrived_lists


GROUP = 8


def bin_kernel(slot_ref, offs_ref, y_ref, cos_ref, sin_ref, out_ref, *, slots):
    dets, samples = y_ref.shape
    blocks = slot_ref.shape[0] // dets
    tile = samples // blocks
    out_ref[...] = jnp.zeros(out_ref.shape, out_ref.dtype)
    half = tile // 2
    pix = lax.broadcasted_iota(jnp.int32, (half, tile), 0)

    for first in range(0, dets, GROUP):
        def body(blk, carry):
            start = pl.multiple_of(blk * tile, tile)
            cols = pl.ds(start, tile)
            y = y_ref[first : first + GROUP, cols]
            offs = offs_ref[first : first + GROUP, cols]
            parts = [y, cos_ref[first : first + GROUP, cols] * y, sin_ref[first : first + GROUP, cols] * y]
            values = jnp.concatenate(parts, axis=0)
            high = values.astype(jnp.bfloat16)
            rest = values - high.astype(jnp.float32)
            mid = rest.astype(jnp.bfloat16)
            low = (rest - mid.astype(jnp.float32)).astype(jnp.bfloat16)
            zero = jnp.zeros((1, tile), jnp.bfloat16)
            for i in range(GROUP):
                upper = offs[i : i + 1] >= half
                pieces = [piece[s * GROUP + i : s * GROUP + i + 1] for piece in (high, mid, low) for s in range(3)]
                stack = jnp.concatenate(
                    [jnp.where(upper, zero, r) for r in pieces]
                    + [jnp.where(upper, r, zero) for r in pieces]
                    + [jnp.zeros((32 - 18, tile), jnp.bfloat16)],
                    axis=0,
                )
                hot = ((offs[i : i + 1] % half) == pix).astype(jnp.bfloat16)
                res = lax.dot_general(
                    stack, hot, (((1,), (1,)), ((), ())), preferred_element_type=jnp.float32
                )
                below = res[0:3] + res[3:6] + res[6:9]
                above = res[9:12] + res[12:15] + res[15:18]
                total = jnp.concatenate([below, above], axis=1)
                h = slot_ref[(first + i) * blocks + blk]
                row = h // slots
                lane = pl.multiple_of((h % slots) * (3 * tile), 128)
                for s in range(3):
                    spot = (pl.ds(row, 1), pl.ds(lane + s * tile, tile))
                    out_ref[spot] = out_ref[spot] + total[s : s + 1]
            return carry

        lax.fori_loop(0, blocks, body, 0)


def bin_call(slot_ids, offs, y, cos, sin, hit_total, tile, slots):
    return pl.pallas_call(
        functools.partial(bin_kernel, slots=slots),
        out_shape=jax.ShapeDtypeStruct((hit_total // slots, slots * 3 * tile), jnp.float32),
        grid_spec=pltpu.PrefetchScalarGridSpec(
            num_scalar_prefetch=1,
            grid=(1,),
            in_specs=[pl.BlockSpec(memory_space=pltpu.VMEM)] * 4,
            out_specs=pl.BlockSpec(memory_space=pltpu.VMEM),
        ),
    )(slot_ids, offs, y, cos, sin)


def read_kernel(slot_ref, maps_ref, offs_ref, cos_ref, sin_ref, out_ref):
    lanes = 128
    dets, samples = offs_ref.shape
    blocks = slot_ref.shape[0] // dets
    tile = maps_ref.shape[1] // 3

    for first in range(0, dets, GROUP):
        def body(blk, carry):
            rows = jnp.concatenate(
                [maps_ref[pl.ds(slot_ref[(first + i) * blocks + blk], 1), :] for i in range(GROUP)],
                axis=0,
            )
            for j in range(tile // lanes):
                start = pl.multiple_of(blk * tile + j * lanes, lanes)
                cols = pl.ds(start, lanes)
                idx = offs_ref[first : first + GROUP, cols]
                low = idx % lanes
                upper = idx >= lanes
                picked = []
                for s in range(3):
                    a = jnp.take_along_axis(
                        rows[:, s * tile : s * tile + lanes], low, axis=1, mode="promise_in_bounds"
                    )
                    b = jnp.take_along_axis(
                        rows[:, s * tile + lanes : (s + 1) * tile], low, axis=1, mode="promise_in_bounds"
                    )
                    picked.append(jnp.where(upper, b, a))
                c = cos_ref[first : first + GROUP, cols]
                sn = sin_ref[first : first + GROUP, cols]
                out_ref[first : first + GROUP, cols] = picked[0] + c * picked[1] + sn * picked[2]
            return carry

        lax.fori_loop(0, blocks, body, 0)


def read_call(slots, maps, offs, cos, sin):
    return pl.pallas_call(
        read_kernel,
        out_shape=jax.ShapeDtypeStruct(offs.shape, jnp.float32),
        grid_spec=pltpu.PrefetchScalarGridSpec(
            num_scalar_prefetch=1,
            grid=(1,),
            in_specs=[pl.BlockSpec(memory_space=pltpu.VMEM)] * 4,
            out_specs=pl.BlockSpec(memory_space=pltpu.VMEM),
        ),
    )(slots, maps, offs, cos, sin)


def local(tod, det_angle, angle_index, offsets, block_slot, hit_tiles, noise_filter, precond):
    shards = lax.axis_size(("tod", "map"))
    hits = hit_tiles[0]
    slot_count = hits.shape[1]
    tiles_dev = precond.shape[0]
    tile_pix = precond.shape[2]
    det_count, samp_count = tod.shape
    blocks_per_det = block_slot.shape[1]
    block_len = samp_count // blocks_per_det
    block_total = det_count * blocks_per_det
    hit_total = shards * slot_count
    highest = lax.Precision.HIGH
    psi = det_angle[:, None] + jnp.pi * angle_index.astype(jnp.float32) / ANGLES
    cosine = jnp.cos(2.0 * psi)
    sine = jnp.sin(2.0 * psi)

    band = noise_filter.shape[1] - 1
    rows = jnp.arange(3 * band, dtype=jnp.int32)[:, None]
    cols = jnp.arange(band, dtype=jnp.int32)[None, :]
    lag = jnp.abs(rows - cols - band)
    lag_hot = (lag[:, :, None] == jnp.arange(band + 1, dtype=jnp.int32)[None, None, :]).astype(
        jnp.bfloat16
    )
    taps_high = lax.reduce_precision(noise_filter, exponent_bits=8, mantissa_bits=7)
    taps_rest = noise_filter - taps_high
    taps_mid = lax.reduce_precision(taps_rest, exponent_bits=8, mantissa_bits=7)
    taps_low = lax.reduce_precision(taps_rest - taps_mid, exponent_bits=8, mantissa_bits=7)
    toeplitz = jnp.einsum(
        "pdk,rck->pdrc",
        jnp.stack([taps_high, taps_mid, taps_low]).astype(jnp.bfloat16),
        lag_hot,
        preferred_element_type=jnp.float32,
    ).sum(axis=0)
    block_count = samp_count // band

    def weigh(stream):
        padded = extended(stream, (("tod", 1),), band).reshape(det_count, block_count + 2, band)
        stacked = jnp.concatenate(
            [padded[:, k : k + block_count] for k in range(3)], axis=2
        )
        out = jnp.einsum(
            "dbj,dji->dbi",
            stacked,
            toeplitz,
            precision=highest,
            preferred_element_type=jnp.float32,
        )
        return out.reshape(det_count, samp_count)

    def owner_sum(arrived, owner_flat, owner_index):
        kept = jnp.where((owner_flat >= 0)[:, None], arrived.reshape(hit_total, 3 * tile_pix), 0.0)
        summed = jnp.zeros((tiles_dev, 3 * tile_pix), jnp.float32).at[owner_index].add(kept)
        return summed

    def binning(stream, partial):
        touched = bin_call(block_slot.reshape(-1), offsets, stream, cosine, sine, hit_total, tile_pix, slot_count)
        arrived, total = exchange(touched.reshape(shards, slot_count * 3 * tile_pix), partial)
        return owner_sum(arrived, owner_flat, owner_index), total

    def projection(field, partial):
        outgoing = jnp.where(
            (owner_flat >= 0)[:, None],
            jnp.take(field, owner_index, axis=0),
            0.0,
        )
        touched, total = exchange(outgoing.reshape(shards, slot_count * 3 * tile_pix), partial)
        stream = read_call(
            block_slot.reshape(-1), touched.reshape(hit_total, 3 * tile_pix), offsets, cosine, sine
        )
        return stream.reshape(det_count, samp_count), total

    touched = bin_call(block_slot.reshape(-1), offsets, weigh(tod), cosine, sine, hit_total, tile_pix, slot_count)
    arrived, _, owner_lists = exchange(
        touched.reshape(shards, slot_count * 3 * tile_pix), None, hits
    )
    owner_flat = owner_lists.reshape(-1)
    owner_index = jnp.clip(owner_flat, 0, tiles_dev - 1)
    rhs = owner_sum(arrived, owner_flat, owner_index)
    solution = jnp.zeros_like(rhs)
    residual = rhs
    zeta = precondition(residual, precond)
    direction = zeta
    stream_dir, norm_now = projection(zeta, jnp.sum(residual * zeta))
    for step in range(ITERS):
        weighed = weigh(stream_dir)
        image, curvature = binning(weighed, jnp.sum(stream_dir * weighed))
        alpha = norm_now / curvature
        solution = solution + alpha * direction
        residual = residual - alpha * image
        if step + 1 < ITERS:
            zeta = precondition(residual, precond)
            stream_zeta, norm_next = projection(zeta, jnp.sum(residual * zeta))
            beta = norm_next / norm_now
            direction = zeta + beta * direction
            stream_dir = stream_zeta + beta * stream_dir
            norm_now = norm_next
    return (solution.reshape(tiles_dev, 3, tile_pix), residual.reshape(tiles_dev, 3, tile_pix))


def solution(mesh):
    in_specs = (
        P("map", "tod"),
        P("map"),
        P("map", "tod"),
        P("map", "tod"),
        P("map", "tod"),
        P(("tod", "map"), None, None),
        P("map", None),
        P(("tod", "map"), None, None),
    )
    out_specs = (P(("tod", "map"), None, None), P(("tod", "map"), None, None))
    return jax.shard_map(local, mesh=mesh, in_specs=in_specs, out_specs=out_specs, check_vma=False)
```

profile of v0, /device:TPU:1, one launch (start us, length us, event | category | flops | bytes accessed | tf_op | source)
XLA Modules:
  0.0 269.8 jit_solution(15469798513287980936)
XLA Ops:
  0.6 0.7 fusion.84
  1.3 3.9 %collective-permute-start = (f32[16,128]{1,0:T(8,128)S(1)}, f32[16,128]{1,0:T(8,128)S(1)}, u32[]{:S(2)}, u32[]{:S(2)}) collective-permute-start(f32[16,128]{1,0:T(8,128)S(1)} %get-tuple-element.34), channel_id=1, source_target_pairs={{0,8},{8,16},{16,24},{24,32},{32,40},{40,48},{48,56},{56,64},{64,7... | collective-permute-start | bytes 24584 | tf_op jit(solution)/shard_map/ppermute | solution.py:23
  5.3 1.3 collective-permute-start.1
  6.6 0.8 convert_bitcast_fusion.1
  7.4 0.7 fusion.69
  8.1 2.7 %fusion.57 = (f32[16,4096]{1,0:T(8,128)}, f32[16,4096]{1,0:T(8,128)}) fusion(s32[16,4096]{1,0:T(8,128)} %param.12, f32[16]{0:T(128)} %param.11), kind=kLoop, calls=%fused_computation.108 | loop fusion | flops 262144 | bytes 786496 | tf_op jit(solution)/shard_map/sin | solution.py:186
  10.9 5.3 %fusion.10 = f32[16,384,128]{2,0,1:T(8,128)S(1)} fusion(s32[384,128]{1,0:T(8,128)S(1)} %add_abs_fusion, bf16[1,16,129]{2,1,0:T(8,128)(2,1)S(1)} %get-tuple-element.37, bf16[1,16,129]{2,1,0:T(8,128)(2,1)S(1)} %get-tuple-element.38, bf16[1,16,129]{2,1,0:T(8,128)(2,1)S(1)} %get-tuple-element.36), kind=kOutput, calls=%fused_computation.15 | convolution fusion | flops 616648960 | bytes 3354720 | tf_op jit(solution)/shard_map/pdk,rck->pdrc/dot_general | solution.py:199
  16.3 0.8 reshape.138.slot_ref
  17.1 0.8 pad_maximum_fusion.5
  18.0 1.0 reshape.139
  19.0 2.4 fusion.8
  21.4 0.9 copy.55
  22.3 13.3 %shard_map.95 = f32[128,1536]{1,0:T(8,128)} custom-call(s32[256]{0:T(256)} %reshape.138.slot_ref, s32[16,4096]{1,0:T(8,128)} %offs_ref.9, f32[16,4096]{1,0:T(8,128)} %bitcast.163, f32[16,4096]{1,0:T(8,128)} %get-tuple-element.29.cos_ref, f32[16,4096]{1,0:T(8,128)} %get-tuple-element.28.sin_ref), custom_call_target="tpu_custom_call" | custom-call | tf_op jit(solution)/shard_map/pallas_call | solution.py:112
  35.5 1.2 maximum_bitcast_fusion
  36.7 0.9 copy.14
  37.6 28.7 %all_to_all.60 = f32[128,1,1664]{2,1,0:T(1,128)S(1)} all-to-all(f32[128,1,1664]{2,1,0:T(1,128)S(1)} %copy.14), channel_id=1, replica_groups=mesh['tod'=16,'map'=8] {'tod','map'}, dimensions={0} | all-to-all | bytes 1703936 | tf_op jit(solution)/shard_map/all_to_all | solution.py:51
  67.1 1.0 reshape.141
  68.1 3.4 %scatter_custom_fusion = f32[384,768]{1,0:T(8,128)S(1)} fusion(s32[256]{0:T(256)S(1)} %bitcast.165, f32[256,768]{1,0:T(8,128)} %reshape.141, f32[]{:T(128)} %constant.18.clone.1, pred[256]{0:T(512)(128)(4,1)S(1)} %ge.20), kind=kCustom, calls=%fused_computation.57 | custom fusion | flops 393216 | bytes 1967616 | tf_op jit(solution)/shard_map/scatter-add | solution.py:223
  71.8 0.7 copy-done.3
  72.6 0.9 multiply_reduce_fusion.1
  73.5 1.1 gather_fusion
  76.3 21.3 %all_to_all.61 = f32[128,1,1664]{2,1,0:T(1,128)S(1)} all-to-all(f32[128,1,1664]{2,1,0:T(1,128)S(1)} %all_to_all.43), channel_id=1, replica_groups=mesh['tod'=16,'map'=8] {'tod','map'}, dimensions={0} | all-to-all | bytes 1703936 | tf_op jit(solution)/shard_map/all_to_all | solution.py:51
  97.7 0.9 copy-done.22
  98.6 1.0 reshape.143.maps_ref
  99.6 6.4 %shard_map.96 = f32[16,4096]{1,0:T(8,128)} custom-call(s32[256]{0:T(256)} %reshape.138.slot_ref, f32[256,768]{1,0:T(8,128)} %reshape.143.maps_ref, s32[16,4096]{1,0:T(8,128)} %offs_ref.9, f32[16,4096]{1,0:T(8,128)} %get-tuple-element.29.cos_ref, f32[16,4096]{1,0:T(8,128)} %get-tuple-element.28.sin_ref), custom_call_target="tpu_custom_call" | custom-call | tf_op jit(solution)/shard_map/pallas_call | solution.py:160
  106.0 0.7 fusion.83
  106.7 2.3 collective-permute-start.2
  109.1 1.3 collective-permute-start.3
  110.4 3.1 %collective-permute-done.3 = f32[16,128]{1,0:T(8,128)S(1)} collective-permute-done((f32[16,128]{1,0:T(8,128)S(1)}, f32[16,128]{1,0:T(8,128)S(1)}, u32[]{:S(2)}, u32[]{:S(2)}) %collective-permute-start.3) | collective-permute-done | bytes 8224 | tf_op jit(solution)/shard_map/ppermute | solution.py:25
  113.5 1.7 pad_maximum_fusion.6
  115.2 1.0 reshape.144
  116.3 2.4 fusion.6
  118.7 0.8 multiply_reduce_fusion.3
  119.4 0.9 copy.54
  120.9 13.3 %shard_map.97 = f32[128,1536]{1,0:T(8,128)} custom-call(s32[256]{0:T(256)} %reshape.138.slot_ref, s32[16,4096]{1,0:T(8,128)} %offs_ref.9, f32[16,4096]{1,0:T(8,128)} %bitcast.160, f32[16,4096]{1,0:T(8,128)} %get-tuple-element.29.cos_ref, f32[16,4096]{1,0:T(8,128)} %get-tuple-element.28.sin_ref), custom_call_target="tpu_custom_call" | custom-call | tf_op jit(solution)/shard_map/pallas_call | solution.py:112
  134.2 1.2 maximum_bitcast_fusion.1
  135.4 1.8 copy.16
  137.2 9.4 %all-to-all-start.2 = ((f32[128,1,1664]{2,1,0:T(1,128)}), f32[128,1,1664]{2,1,0:T(1,128)S(1)}, u32[]{:S(2)}, u32[]{:S(2)}) async-start(f32[128,1,1664]{2,1,0:T(1,128)} %copy.16), calls=%async_computation.2 | async-start | bytes 1703936 | tf_op jit(solution)/shard_map/all_to_all | solution.py:51
  146.6 1.5 slice_reduce_fusion.3
  148.0 15.4 %all-to-all-done.2 = f32[128,1,1664]{2,1,0:T(1,128)S(1)} async-done(((f32[128,1,1664]{2,1,0:T(1,128)}), f32[128,1,1664]{2,1,0:T(1,128)S(1)}, u32[]{:S(2)}, u32[]{:S(2)}) %all-to-all-start.2) | async-done | bytes 852000 | tf_op jit(solution)/shard_map/all_to_all | solution.py:51
  164.3 2.8 %scatter_custom_fusion.1 = f32[384,768]{1,0:T(8,128)S(1)} fusion(s32[256]{0:T(256)S(1)} %bitcast.166, f32[256,768]{1,0:T(8,128)S(1)} %reshape.146, f32[]{:T(128)} %constant.18.clone.1, pred[256]{0:T(512)(128)(4,1)S(1)} %ge.20), kind=kCustom, calls=%fused_computation.55 | custom fusion | flops 393216 | bytes 1967616 | tf_op jit(solution)/shard_map/scatter-add | solution.py:223
  168.6 1.5 copy-done.8
  170.3 0.7 copy-done.5
  171.1 0.9 multiply_reduce_fusion
  172.0 1.1 gather_fusion.1
  174.8 21.3 %all_to_all.62 = f32[128,1,1664]{2,1,0:T(1,128)S(1)} all-to-all(f32[128,1,1664]{2,1,0:T(1,128)S(1)} %all_to_all.49), channel_id=1, replica_groups=mesh['tod'=16,'map'=8] {'tod','map'}, dimensions={0} | all-to-all | bytes 1703936 | tf_op jit(solution)/shard_map/all_to_all | solution.py:51
  198.2 1.0 reshape.148.maps_ref
  199.2 6.2 %shard_map.98 = f32[16,4096]{1,0:T(8,128)} custom-call(s32[256]{0:T(256)} %reshape.138.slot_ref, f32[256,768]{1,0:T(8,128)} %reshape.148.maps_ref, s32[16,4096]{1,0:T(8,128)} %offs_ref.9, f32[16,4096]{1,0:T(8,128)} %get-tuple-element.29.cos_ref, f32[16,4096]{1,0:T(8,128)} %get-tuple-element.28.sin_ref), custom_call_target="tpu_custom_call" | custom-call | tf_op jit(solution)/shard_map/pallas_call | solution.py:160
  205.3 1.1 multiply_add_fusion
  206.5 2.3 collective-permute-start.4
  208.8 1.3 collective-permute-start.5
  210.1 3.1 %collective-permute-done.5 = f32[16,128]{1,0:T(8,128)S(1)} collective-permute-done((f32[16,128]{1,0:T(8,128)S(1)}, f32[16,128]{1,0:T(8,128)S(1)}, u32[]{:S(2)}, u32[]{:S(2)}) %collective-permute-start.5) | collective-permute-done | bytes 8224 | tf_op jit(solution)/shard_map/ppermute | solution.py:25
  213.2 0.7 pad_maximum_fusion.7
  213.9 1.0 reshape.149
  215.0 2.4 fusion.4
  217.4 0.8 multiply_reduce_fusion.2
  218.3 0.9 copy.53
  219.1 13.3 %shard_map.99 = f32[128,1536]{1,0:T(8,128)} custom-call(s32[256]{0:T(256)} %reshape.138.slot_ref, s32[16,4096]{1,0:T(8,128)} %offs_ref.9, f32[16,4096]{1,0:T(8,128)} %bitcast.161, f32[16,4096]{1,0:T(8,128)} %get-tuple-element.29.cos_ref, f32[16,4096]{1,0:T(8,128)} %get-tuple-element.28.sin_ref), custom_call_target="tpu_custom_call" | custom-call | tf_op jit(solution)/shard_map/pallas_call | solution.py:112
  233.1 1.2 maximum_bitcast_fusion.2
  234.3 0.9 copy.18
  235.2 26.0 %all_to_all.63 = f32[128,1,1664]{2,1,0:T(1,128)S(1)} all-to-all(f32[128,1,1664]{2,1,0:T(1,128)S(1)} %copy.18), channel_id=1, replica_groups=mesh['tod'=16,'map'=8] {'tod','map'}, dimensions={0} | all-to-all | bytes 1703936 | tf_op jit(solution)/shard_map/all_to_all | solution.py:51
  263.4 2.6 scatter_custom_fusion.2
  266.6 1.4 copy.20
  268.6 1.2 fusion.14
  (106 shorter events, 10.2 us)
Async XLA Ops:
  1.3 15.8 %collective-permute-start = (f32[16,128]{1,0:T(8,128)S(1)}, f32[16,128]{1,0:T(8,128)S(1)}, u32[]{:S(2)}, u32[]{:S(2)}) collective-permute-start(f32[16,128]{1,0:T(8,128)S(1)} %get-tuple-element.34), channel_id=1, source_target_pairs={{0,8},{8,16},{16,24},{24,32},{32,40},{40,48},{48,56},{56,64},{64,7... | collective-permute-start | bytes 24584 | tf_op jit(solution)/shard_map/ppermute | solution.py:23
  5.3 11.8 %collective-permute-start.1 = (f32[16,128]{1,0:T(8,128)S(1)}, f32[16,128]{1,0:T(8,128)S(1)}, u32[]{:S(2)}, u32[]{:S(2)}) collective-permute-start(f32[16,128]{1,0:T(8,128)S(1)} %get-tuple-element.35), channel_id=1, source_target_pairs={{8,0},{16,8},{24,16},{32,24},{40,32},{48,40},{56,48},{64,56},{72,6... | collective-permute-start | bytes 24584 | tf_op jit(solution)/shard_map/ppermute | solution.py:25
  10.9 5.5 %copy-start.26 = (s32[16,16]{1,0:T(8,128)S(1)}, s32[16,16]{1,0:T(8,128)}, u32[]{:S(2)}) copy-start(s32[16,16]{1,0:T(8,128)} %param.14) | copy-start | bytes 3076
  10.9 6.3 %copy-start.25 = (f32[16,4096]{1,0:T(8,128)S(1)}, f32[16,4096]{1,0:T(8,128)}, u32[]{:S(2)}) copy-start(f32[16,4096]{1,0:T(8,128)} %param.10) | copy-start | bytes 786436
  16.2 6.1 %copy-start = (f32[16,384,128]{2,0,1:T(8,128)}, f32[16,384,128]{2,0,1:T(8,128)S(1)}, u32[]{:S(2)}) copy-start(f32[16,384,128]{2,0,1:T(8,128)S(1)} %fusion.10) | copy-start | bytes 9437188
  67.1 4.4 %copy-start.7 = (f32[384,6,256]{2,0,1:T(8,128)S(1)}, f32[384,6,256]{2,0,1:T(8,128)}, u32[]{:S(2)}) copy-start(f32[384,6,256]{2,0,1:T(8,128)} %param.17) | copy-start | bytes 7077892
  71.6 1.0 copy-start.3
  71.8 1.7 copy-start.10
  71.8 1.7 copy-start.12
  71.8 1.7 copy-start.14
  97.6 0.9 copy-start.22
  99.6 16.6 %copy-start.1 = (f32[16,384,128]{2,0,1:T(8,128)S(1)}, f32[16,384,128]{2,0,1:T(8,128)}, u32[]{:S(2)}) copy-start(f32[16,384,128]{2,0,1:T(8,128)} %copy-done) | copy-start | bytes 9437188
  106.7 3.6 %collective-permute-start.2 = (f32[16,128]{1,0:T(8,128)S(1)}, f32[16,128]{1,0:T(8,128)S(1)}, u32[]{:S(2)}, u32[]{:S(2)}) collective-permute-start(f32[16,128]{1,0:T(8,128)S(1)} %get-tuple-element.32), channel_id=1, source_target_pairs={{0,8},{8,16},{16,24},{24,32},{32,40},{40,48},{48,56},{56,64},{64,7... | collective-permute-start | bytes 24584 | tf_op jit(solution)/shard_map/ppermute | solution.py:23
  109.1 4.4 %collective-permute-start.3 = (f32[16,128]{1,0:T(8,128)S(1)}, f32[16,128]{1,0:T(8,128)S(1)}, u32[]{:S(2)}, u32[]{:S(2)}) collective-permute-start(f32[16,128]{1,0:T(8,128)S(1)} %get-tuple-element.33), channel_id=1, source_target_pairs={{8,0},{16,8},{24,16},{32,24},{40,32},{48,40},{56,48},{64,56},{72,6... | collective-permute-start | bytes 24584 | tf_op jit(solution)/shard_map/ppermute | solution.py:25
  116.3 2.4 copy-start.9
  137.2 26.2 %all-to-all-start.2 = ((f32[128,1,1664]{2,1,0:T(1,128)}), f32[128,1,1664]{2,1,0:T(1,128)S(1)}, u32[]{:S(2)}, u32[]{:S(2)}) async-start(f32[128,1,1664]{2,1,0:T(1,128)} %copy.16), calls=%async_computation.2 | async-start | bytes 1703936 | tf_op jit(solution)/shard_map/all_to_all | solution.py:51
  164.3 4.1 %copy-start.4 = (f32[384,768]{1,0:T(8,128)S(1)}, f32[384,768]{1,0:T(8,128)}, u32[]{:S(2)}) copy-start(f32[384,768]{1,0:T(8,128)} %copy-done.3) | copy-start | bytes 3538948
  168.4 1.7 copy-start.8
  170.1 1.0 copy-start.5
  170.3 1.7 copy-start.16
  170.3 1.7 copy-start.18
  170.3 1.7 copy-start.20
  205.3 9.7 %copy-start.2 = (f32[16,384,128]{2,0,1:T(8,128)S(1)}, f32[16,384,128]{2,0,1:T(8,128)}, u32[]{:S(2)}) copy-start(f32[16,384,128]{2,0,1:T(8,128)} %copy-done) | copy-start | bytes 9437188
  206.4 6.8 %copy-start.23 = (f32[16,4096]{1,0:T(8,128)}, f32[16,4096]{1,0:T(8,128)S(1)}, u32[]{:S(2)}) copy-start(f32[16,4096]{1,0:T(8,128)S(1)} %multiply_add_fusion) | copy-start | bytes 786436
  206.5 3.7 %collective-permute-start.4 = (f32[16,128]{1,0:T(8,128)S(1)}, f32[16,128]{1,0:T(8,128)S(1)}, u32[]{:S(2)}, u32[]{:S(2)}) collective-permute-start(f32[16,128]{1,0:T(8,128)S(1)} %get-tuple-element.30), channel_id=1, source_target_pairs={{0,8},{8,16},{16,24},{24,32},{32,40},{40,48},{48,56},{56,64},{64,7... | collective-permute-start | bytes 24584 | tf_op jit(solution)/shard_map/ppermute | solution.py:23
  208.8 4.4 %collective-permute-start.5 = (f32[16,128]{1,0:T(8,128)S(1)}, f32[16,128]{1,0:T(8,128)S(1)}, u32[]{:S(2)}, u32[]{:S(2)}) collective-permute-start(f32[16,128]{1,0:T(8,128)S(1)} %get-tuple-element.31), channel_id=1, source_target_pairs={{8,0},{16,8},{24,16},{32,24},{40,32},{48,40},{56,48},{64,56},{72,6... | collective-permute-start | bytes 24584 | tf_op jit(solution)/shard_map/ppermute | solution.py:25
  215.0 2.4 copy-start.24
  263.4 2.6 copy-start.6
  266.6 1.4 copy-start.11
  266.6 1.4 copy-start.13
  266.6 1.4 copy-start.15
  266.6 1.4 copy-start.17
  266.6 1.8 copy-start.19
  266.6 2.0 copy-start.21
where the time goes:
time: 271 us; the launch traced here: 270 us
  blocking collectives  97.3 us (36%)
  Pallas kernels  52.3 us (19%)
  other arithmetic  33.2 us (12%)
  local copies, waits for them, and re-layouts  26 us (10%)
  starting transfers between devices  21.9 us (8%)
  waiting for transfers between devices  21.5 us (8%)
  matrix products  12.4 us (5%)
  between operations  5.19 us (2%)
    all_to_all x4, blocking collectives, exchange(): lax.all_to_all(rows, ('tod', 'map'), split_axis=0, concat_axis=0, tiled=T...  97.3 us
    pallas_call x3, Pallas kernels, bin_call(): pl.pallas_call(functools.partial(bin_kernel, slots=slots), out_shape=jax....  39.8 us
    all_to_all x1, waiting for transfers between devices, exchange(): lax.all_to_all(rows, ('tod', 'map'), split_axis=0, concat_axis=0, tiled=T...  15.4 us
    pallas_call x2, Pallas kernels, read_call(): pl.pallas_call(read_kernel, out_shape=jax.ShapeDtypeStruct(offs.shape, jn...  12.6 us
    all_to_all x1, starting transfers between devices, exchange(): lax.all_to_all(rows, ('tod', 'map'), split_axis=0, concat_axis=0, tiled=T...  9.39 us
    scatter-add x3, other arithmetic, owner_sum(): jnp.zeros((tiles_dev, 3 * tile_pix), jnp.float32).at[owner_index].add(kept)  8.86 us
    unnamed x63, local copies, waits for them, and re-layouts  8.81 us
    ppermute x3, starting transfers between devices, extended(): lax.ppermute(tail, axis, [(i, (i + 1) % count) for i in range(ends)])  8.61 us
  transfers between devices with their start and end apart: 7, of which 3 were waited for; matrix products, arithmetic and copies ran while one was open for 4% of the time, Pallas kernels for 0%

commit v1 on v0

--- a/solution.py
+++ b/solution.py
@@ -219,9 +219,16 @@
         return out.reshape(det_count, samp_count)
 
     def owner_sum(arrived, owner_flat, owner_index):
-        kept = jnp.where((owner_flat >= 0)[:, None], arrived.reshape(hit_total, 3 * tile_pix), 0.0)
-        summed = jnp.zeros((tiles_dev, 3 * tile_pix), jnp.float32).at[owner_index].add(kept)
-        return summed
+        placement = (
+            owner_flat[:, None] == jnp.arange(tiles_dev, dtype=jnp.int32)[None, :]
+        ).astype(jnp.float32)
+        return lax.dot_general(
+            placement,
+            arrived.reshape(hit_total, 3 * tile_pix),
+            (((0,), (0,)), ((), ())),
+            precision=highest,
+            preferred_element_type=jnp.float32,
+        )
 
     def binning(stream, partial):
         touched = bin_call(block_slot.reshape(-1), offsets, stream, cosine, sine, hit_total, tile_pix, slot_count)

time: 271 us -> 264 us (0.974)
  other arithmetic: 33.2 us -> 23.8 us
    scatter-add x3 -> x0, other arithmetic: 8.86 us -> none  [owner_sum(): jnp.zeros((tiles_dev, 3 * tile_pix), jnp.float32).at[owner_index].add(kept)]
  transfers between devices with their start and end apart: 7 -> 7, of which waited for: 3 -> 3; matrix products, arithmetic and copies ran while one was open for 4% -> 5% of each run, Pallas kernels for 0% -> 0%
where the time goes in v1:
time: 264 us; the launch traced here: 263 us
  blocking collectives  97.3 us (37%)
  Pallas kernels  52.3 us (20%)
  local copies, waits for them, and re-layouts  26.6 us (10%)
  other arithmetic  23.8 us (9%)
  starting transfers between devices  22.1 us (8%)
  waiting for transfers between devices  21.3 us (8%)
  matrix products  14.2 us (5%)
  between operations  5.45 us (2%)
    all_to_all x4, blocking collectives, exchange(): lax.all_to_all(rows, ('tod', 'map'), split_axis=0, concat_axis=0, tiled=T...  97.3 us
    pallas_call x3, Pallas kernels, bin_call(): pl.pallas_call(functools.partial(bin_kernel, slots=slots), out_shape=jax....  39.8 us
    all_to_all x1, waiting for transfers between devices, exchange(): lax.all_to_all(rows, ('tod', 'map'), split_axis=0, concat_axis=0, tiled=T...  15.3 us
    pallas_call x2, Pallas kernels, read_call(): pl.pallas_call(read_kernel, out_shape=jax.ShapeDtypeStruct(offs.shape, jn...  12.6 us
    all_to_all x1, starting transfers between devices, exchange(): lax.all_to_all(rows, ('tod', 'map'), split_axis=0, concat_axis=0, tiled=T...  9.39 us
    ppermute x3, starting transfers between devices, extended(): lax.ppermute(tail, axis, [(i, (i + 1) % count) for i in range(ends)])  8.61 us
    unnamed x63, local copies, waits for them, and re-layouts  8.36 us
    dot_general x3, matrix products, weigh(): jnp.einsum('dbj,dji->dbi', stacked, toeplitz, precision=highest, preferre...  7.1 us
  transfers between devices with their start and end apart: 7, of which 3 were waited for; matrix products, arithmetic and copies ran while one was open for 5% of the time, Pallas kernels for 0%

profile of v1, /device:TPU:1, one launch (start us, length us, event | category | flops | bytes accessed | tf_op | source)
XLA Modules:
  0.0 263.1 jit_solution(13220625667956752135)
XLA Ops:
  0.6 0.7 fusion.73
  1.3 3.9 %collective-permute-start = (f32[16,128]{1,0:T(8,128)S(1)}, f32[16,128]{1,0:T(8,128)S(1)}, u32[]{:S(2)}, u32[]{:S(2)}) collective-permute-start(f32[16,128]{1,0:T(8,128)S(1)} %get-tuple-element.34), channel_id=1, source_target_pairs={{0,8},{8,16},{16,24},{24,32},{32,40},{40,48},{48,56},{56,64},{64,7... | collective-permute-start | bytes 24584 | tf_op jit(solution)/shard_map/ppermute | solution.py:23
  5.3 1.3 collective-permute-start.1
  6.6 0.8 convert_bitcast_fusion.1
  7.4 0.7 fusion.58
  8.1 2.7 %fusion.45 = (f32[16,4096]{1,0:T(8,128)}, f32[16,4096]{1,0:T(8,128)}) fusion(s32[16,4096]{1,0:T(8,128)} %param.12, f32[16]{0:T(128)} %param.11), kind=kLoop, calls=%fused_computation.94 | loop fusion | flops 262144 | bytes 786496 | tf_op jit(solution)/shard_map/sin | solution.py:186
  10.9 5.3 %fusion.10 = f32[16,384,128]{2,0,1:T(8,128)S(1)} fusion(s32[384,128]{1,0:T(8,128)S(1)} %add_abs_fusion, bf16[1,16,129]{2,1,0:T(8,128)(2,1)S(1)} %get-tuple-element.37, bf16[1,16,129]{2,1,0:T(8,128)(2,1)S(1)} %get-tuple-element.38, bf16[1,16,129]{2,1,0:T(8,128)(2,1)S(1)} %get-tuple-element.36), kind=kOutput, calls=%fused_computation.12 | convolution fusion | flops 616648960 | bytes 3354720 | tf_op jit(solution)/shard_map/pdk,rck->pdrc/dot_general | solution.py:199
  16.3 0.8 reshape.114.slot_ref
  17.2 0.8 pad_maximum_fusion.5
  18.0 1.0 reshape.115
  19.1 2.4 fusion.8
  21.4 0.9 copy.55
  22.3 13.3 %shard_map.95 = f32[128,1536]{1,0:T(8,128)} custom-call(s32[256]{0:T(256)} %reshape.114.slot_ref, s32[16,4096]{1,0:T(8,128)} %offs_ref.9, f32[16,4096]{1,0:T(8,128)} %bitcast.164, f32[16,4096]{1,0:T(8,128)} %get-tuple-element.29.cos_ref, f32[16,4096]{1,0:T(8,128)} %get-tuple-element.28.sin_ref), custom_call_target="tpu_custom_call" | custom-call | tf_op jit(solution)/shard_map/pallas_call | solution.py:112
  35.5 1.2 maximum_bitcast_fusion
  36.7 0.9 copy.14
  37.6 28.7 %all_to_all.60 = f32[128,1,1664]{2,1,0:T(1,128)S(1)} all-to-all(f32[128,1,1664]{2,1,0:T(1,128)S(1)} %copy.14), channel_id=1, replica_groups=mesh['tod'=16,'map'=8] {'tod','map'}, dimensions={0} | all-to-all | bytes 1703936 | tf_op jit(solution)/shard_map/all_to_all | solution.py:51
  66.5 1.0 slice.176
  67.6 1.4 reshape.118
  70.0 0.7 copy-done.5
  70.7 0.9 multiply_reduce_fusion.1
  71.6 1.1 gather_fusion
  73.1 0.7 fusion.63
  74.4 21.3 %all_to_all.61 = f32[128,1,1664]{2,1,0:T(1,128)S(1)} all-to-all(f32[128,1,1664]{2,1,0:T(1,128)S(1)} %all_to_all.43), channel_id=1, replica_groups=mesh['tod'=16,'map'=8] {'tod','map'}, dimensions={0} | all-to-all | bytes 1703936 | tf_op jit(solution)/shard_map/all_to_all | solution.py:51
  95.8 0.9 copy-done.22
  96.8 1.0 reshape.120.maps_ref
  97.8 6.4 %shard_map.96 = f32[16,4096]{1,0:T(8,128)} custom-call(s32[256]{0:T(256)} %reshape.114.slot_ref, f32[256,768]{1,0:T(8,128)} %reshape.120.maps_ref, s32[16,4096]{1,0:T(8,128)} %offs_ref.9, f32[16,4096]{1,0:T(8,128)} %get-tuple-element.29.cos_ref, f32[16,4096]{1,0:T(8,128)} %get-tuple-element.28.sin_ref), custom_call_target="tpu_custom_call" | custom-call | tf_op jit(solution)/shard_map/pallas_call | solution.py:160
  104.2 0.7 fusion.72
  104.9 2.3 collective-permute-start.2
  107.3 1.3 collective-permute-start.3
  108.6 3.1 %collective-permute-done.3 = f32[16,128]{1,0:T(8,128)S(1)} collective-permute-done((f32[16,128]{1,0:T(8,128)S(1)}, f32[16,128]{1,0:T(8,128)S(1)}, u32[]{:S(2)}, u32[]{:S(2)}) %collective-permute-start.3) | collective-permute-done | bytes 8224 | tf_op jit(solution)/shard_map/ppermute | solution.py:25
  111.7 1.7 pad_maximum_fusion.6
  113.3 1.0 reshape.121
  114.4 2.4 fusion.6
  116.8 0.8 multiply_reduce_fusion.3
  117.6 0.9 copy.54
  119.1 13.3 %shard_map.97 = f32[128,1536]{1,0:T(8,128)} custom-call(s32[256]{0:T(256)} %reshape.114.slot_ref, s32[16,4096]{1,0:T(8,128)} %offs_ref.9, f32[16,4096]{1,0:T(8,128)} %bitcast.161, f32[16,4096]{1,0:T(8,128)} %get-tuple-element.29.cos_ref, f32[16,4096]{1,0:T(8,128)} %get-tuple-element.28.sin_ref), custom_call_target="tpu_custom_call" | custom-call | tf_op jit(solution)/shard_map/pallas_call | solution.py:112
  132.4 1.2 maximum_bitcast_fusion.1
  133.6 1.8 copy.16
  135.4 9.4 %all-to-all-start.2 = ((f32[128,1,1664]{2,1,0:T(1,128)}), f32[128,1,1664]{2,1,0:T(1,128)S(1)}, u32[]{:S(2)}, u32[]{:S(2)}) async-start(f32[128,1,1664]{2,1,0:T(1,128)} %copy.16), calls=%async_computation.2 | async-start | bytes 1703936 | tf_op jit(solution)/shard_map/all_to_all | solution.py:51
  144.8 1.5 slice_reduce_fusion.3
  146.2 15.3 %all-to-all-done.2 = f32[128,1,1664]{2,1,0:T(1,128)S(1)} async-done(((f32[128,1,1664]{2,1,0:T(1,128)}), f32[128,1,1664]{2,1,0:T(1,128)S(1)}, u32[]{:S(2)}, u32[]{:S(2)}) %all-to-all-start.2) | async-done | bytes 852000 | tf_op jit(solution)/shard_map/all_to_all | solution.py:51
  164.5 1.0 copy-done.8
  165.8 0.7 copy-done.3
  166.6 0.9 multiply_reduce_fusion
  167.5 1.1 gather_fusion.1
  169.0 0.7 fusion.61
  170.3 21.3 %all_to_all.62 = f32[128,1,1664]{2,1,0:T(1,128)S(1)} all-to-all(f32[128,1,1664]{2,1,0:T(1,128)S(1)} %all_to_all.49), channel_id=1, replica_groups=mesh['tod'=16,'map'=8] {'tod','map'}, dimensions={0} | all-to-all | bytes 1703936 | tf_op jit(solution)/shard_map/all_to_all | solution.py:51
  193.6 1.0 reshape.125.maps_ref
  194.6 6.1 %shard_map.98 = f32[16,4096]{1,0:T(8,128)} custom-call(s32[256]{0:T(256)} %reshape.114.slot_ref, f32[256,768]{1,0:T(8,128)} %reshape.125.maps_ref, s32[16,4096]{1,0:T(8,128)} %offs_ref.9, f32[16,4096]{1,0:T(8,128)} %get-tuple-element.29.cos_ref, f32[16,4096]{1,0:T(8,128)} %get-tuple-element.28.sin_ref), custom_call_target="tpu_custom_call" | custom-call | tf_op jit(solution)/shard_map/pallas_call | solution.py:160
  200.8 1.1 multiply_add_fusion
  201.9 2.3 collective-permute-start.4
  204.3 1.5 collective-permute-start.5
  205.8 2.9 %collective-permute-done.5 = f32[16,128]{1,0:T(8,128)S(1)} collective-permute-done((f32[16,128]{1,0:T(8,128)S(1)}, f32[16,128]{1,0:T(8,128)S(1)}, u32[]{:S(2)}, u32[]{:S(2)}) %collective-permute-start.5) | collective-permute-done | bytes 8224 | tf_op jit(solution)/shard_map/ppermute | solution.py:25
  208.7 0.7 pad_maximum_fusion.7
  209.4 1.0 reshape.126
  210.5 2.4 fusion.4
  212.9 0.8 multiply_reduce_fusion.2
  213.7 0.9 copy.53
  214.5 13.3 %shard_map.99 = f32[128,1536]{1,0:T(8,128)} custom-call(s32[256]{0:T(256)} %reshape.114.slot_ref, s32[16,4096]{1,0:T(8,128)} %offs_ref.9, f32[16,4096]{1,0:T(8,128)} %bitcast.162, f32[16,4096]{1,0:T(8,128)} %get-tuple-element.29.cos_ref, f32[16,4096]{1,0:T(8,128)} %get-tuple-element.28.sin_ref), custom_call_target="tpu_custom_call" | custom-call | tf_op jit(solution)/shard_map/pallas_call | solution.py:112
  228.5 1.2 maximum_bitcast_fusion.2
  229.7 0.9 copy.18
  230.5 26.0 %all_to_all.63 = f32[128,1,1664]{2,1,0:T(1,128)S(1)} all-to-all(f32[128,1,1664]{2,1,0:T(1,128)S(1)} %copy.18), channel_id=1, replica_groups=mesh['tod'=16,'map'=8] {'tod','map'}, dimensions={0} | all-to-all | bytes 1703936 | tf_op jit(solution)/shard_map/all_to_all | solution.py:51
  259.9 1.4 copy.20
  261.9 1.2 fusion.16
  (100 shorter events, 9.9 us)
Async XLA Ops:
  1.3 15.8 %collective-permute-start = (f32[16,128]{1,0:T(8,128)S(1)}, f32[16,128]{1,0:T(8,128)S(1)}, u32[]{:S(2)}, u32[]{:S(2)}) collective-permute-start(f32[16,128]{1,0:T(8,128)S(1)} %get-tuple-element.34), channel_id=1, source_target_pairs={{0,8},{8,16},{16,24},{24,32},{32,40},{40,48},{48,56},{56,64},{64,7... | collective-permute-start | bytes 24584 | tf_op jit(solution)/shard_map/ppermute | solution.py:23
  5.3 11.9 %collective-permute-start.1 = (f32[16,128]{1,0:T(8,128)S(1)}, f32[16,128]{1,0:T(8,128)S(1)}, u32[]{:S(2)}, u32[]{:S(2)}) collective-permute-start(f32[16,128]{1,0:T(8,128)S(1)} %get-tuple-element.35), channel_id=1, source_target_pairs={{8,0},{16,8},{24,16},{32,24},{40,32},{48,40},{56,48},{64,56},{72,6... | collective-permute-start | bytes 24584 | tf_op jit(solution)/shard_map/ppermute | solution.py:25
  10.9 5.5 %copy-start.26 = (s32[16,16]{1,0:T(8,128)S(1)}, s32[16,16]{1,0:T(8,128)}, u32[]{:S(2)}) copy-start(s32[16,16]{1,0:T(8,128)} %param.14) | copy-start | bytes 3076
  10.9 6.3 %copy-start.25 = (f32[16,4096]{1,0:T(8,128)S(1)}, f32[16,4096]{1,0:T(8,128)}, u32[]{:S(2)}) copy-start(f32[16,4096]{1,0:T(8,128)} %param.10) | copy-start | bytes 786436
  16.2 6.1 %copy-start = (f32[16,384,128]{2,0,1:T(8,128)}, f32[16,384,128]{2,0,1:T(8,128)S(1)}, u32[]{:S(2)}) copy-start(f32[16,384,128]{2,0,1:T(8,128)S(1)} %fusion.10) | copy-start | bytes 9437188
  67.6 2.0 copy-start.7
  69.7 1.0 copy-start.5
  69.9 1.7 copy-start.10
  69.9 1.7 copy-start.12
  70.0 1.7 copy-start.14
  95.8 0.9 copy-start.22
  97.8 16.6 %copy-start.1 = (f32[16,384,128]{2,0,1:T(8,128)S(1)}, f32[16,384,128]{2,0,1:T(8,128)}, u32[]{:S(2)}) copy-start(f32[16,384,128]{2,0,1:T(8,128)} %copy-done) | copy-start | bytes 9437188
  104.9 3.6 %collective-permute-start.2 = (f32[16,128]{1,0:T(8,128)S(1)}, f32[16,128]{1,0:T(8,128)S(1)}, u32[]{:S(2)}, u32[]{:S(2)}) collective-permute-start(f32[16,128]{1,0:T(8,128)S(1)} %get-tuple-element.32), channel_id=1, source_target_pairs={{0,8},{8,16},{16,24},{24,32},{32,40},{40,48},{48,56},{56,64},{64,7... | collective-permute-start | bytes 24584 | tf_op jit(solution)/shard_map/ppermute | solution.py:23
  107.3 4.4 %collective-permute-start.3 = (f32[16,128]{1,0:T(8,128)S(1)}, f32[16,128]{1,0:T(8,128)S(1)}, u32[]{:S(2)}, u32[]{:S(2)}) collective-permute-start(f32[16,128]{1,0:T(8,128)S(1)} %get-tuple-element.33), channel_id=1, source_target_pairs={{8,0},{16,8},{24,16},{32,24},{40,32},{48,40},{56,48},{64,56},{72,6... | collective-permute-start | bytes 24584 | tf_op jit(solution)/shard_map/ppermute | solution.py:25
  114.4 2.4 copy-start.9
  135.4 26.2 %all-to-all-start.2 = ((f32[128,1,1664]{2,1,0:T(1,128)}), f32[128,1,1664]{2,1,0:T(1,128)S(1)}, u32[]{:S(2)}, u32[]{:S(2)}) async-start(f32[128,1,1664]{2,1,0:T(1,128)} %copy.16), calls=%async_computation.2 | async-start | bytes 1703936 | tf_op jit(solution)/shard_map/all_to_all | solution.py:51
  162.3 1.5 copy-start.6
  163.9 1.7 copy-start.8
  165.6 1.0 copy-start.3
  165.8 1.7 copy-start.16
  165.8 1.7 copy-start.18
  165.8 1.7 copy-start.20
  200.8 9.7 %copy-start.2 = (f32[16,384,128]{2,0,1:T(8,128)S(1)}, f32[16,384,128]{2,0,1:T(8,128)}, u32[]{:S(2)}) copy-start(f32[16,384,128]{2,0,1:T(8,128)} %copy-done) | copy-start | bytes 9437188
  201.9 6.8 %copy-start.23 = (f32[16,4096]{1,0:T(8,128)}, f32[16,4096]{1,0:T(8,128)S(1)}, u32[]{:S(2)}) copy-start(f32[16,4096]{1,0:T(8,128)S(1)} %multiply_add_fusion) | copy-start | bytes 786436
  201.9 3.9 %collective-permute-start.4 = (f32[16,128]{1,0:T(8,128)S(1)}, f32[16,128]{1,0:T(8,128)S(1)}, u32[]{:S(2)}, u32[]{:S(2)}) collective-permute-start(f32[16,128]{1,0:T(8,128)S(1)} %get-tuple-element.30), channel_id=1, source_target_pairs={{0,8},{8,16},{16,24},{24,32},{32,40},{40,48},{48,56},{56,64},{64,7... | collective-permute-start | bytes 24584 | tf_op jit(solution)/shard_map/ppermute | solution.py:23
  204.3 4.4 %collective-permute-start.5 = (f32[16,128]{1,0:T(8,128)S(1)}, f32[16,128]{1,0:T(8,128)S(1)}, u32[]{:S(2)}, u32[]{:S(2)}) collective-permute-start(f32[16,128]{1,0:T(8,128)S(1)} %get-tuple-element.31), channel_id=1, source_target_pairs={{8,0},{16,8},{24,16},{32,24},{40,32},{48,40},{56,48},{64,56},{72,6... | collective-permute-start | bytes 24584 | tf_op jit(solution)/shard_map/ppermute | solution.py:25
  210.5 2.4 copy-start.24
  257.3 1.5 copy-start.4
  259.8 1.4 copy-start.11
  259.9 1.4 copy-start.13
  259.9 1.4 copy-start.15
  259.9 1.4 copy-start.17
  259.9 1.8 copy-start.19
  259.9 2.0 copy-start.21

commit v2 on v0

--- a/solution.py
+++ b/solution.py
@@ -219,8 +219,21 @@
         return out.reshape(det_count, samp_count)
 
     def owner_sum(arrived, owner_flat, owner_index):
-        kept = jnp.where((owner_flat >= 0)[:, None], arrived.reshape(hit_total, 3 * tile_pix), 0.0)
-        summed = jnp.zeros((tiles_dev, 3 * tile_pix), jnp.float32).at[owner_index].add(kept)
+        width = 3 * tile_pix
+        lists = owner_flat.reshape(shards, slot_count)
+        summed = None
+        for j in range(slot_count):
+            placement = (
+                lists[:, j : j + 1] == jnp.arange(tiles_dev, dtype=jnp.int32)[None, :]
+            ).astype(jnp.float32)
+            part = lax.dot_general(
+                placement,
+                arrived[:, j * width : (j + 1) * width],
+                (((0,), (0,)), ((), ())),
+                precision=highest,
+                preferred_element_type=jnp.float32,
+            )
+            summed = part if summed is None else summed + part
         return summed
 
     def binning(stream, partial):

time: 271 us -> 271 us (level)
  matrix products: 12.4 us -> 20.2 us
  other arithmetic: 33.2 us -> 25.8 us
    scatter-add x3 -> x0, other arithmetic: 8.86 us -> none  [owner_sum(): jnp.zeros((tiles_dev, 3 * tile_pix), jnp.float32).at[owner_index].add(kept)]
    dot_general x0 -> x6, matrix products: none -> 7.75 us  [owner_sum(): lax.dot_general(placement, arrived[:, j * width:(j + 1) * width], (((0,),...]
where the time goes in v2:
time: 271 us; the launch traced here: 270 us
  blocking collectives  97.3 us (36%)
  Pallas kernels  52.3 us (19%)
  local copies, waits for them, and re-layouts  25.9 us (10%)
  other arithmetic  25.8 us (10%)
  starting transfers between devices  21.9 us (8%)
  waiting for transfers between devices  21.5 us (8%)
  matrix products  20.2 us (7%)
  between operations  5.12 us (2%)
    all_to_all x4, blocking collectives, exchange(): lax.all_to_all(rows, ('tod', 'map'), split_axis=0, concat_axis=0, tiled=T...  97.3 us
    pallas_call x3, Pallas kernels, bin_call(): pl.pallas_call(functools.partial(bin_kernel, slots=slots), out_shape=jax....  39.8 us
    all_to_all x1, waiting for transfers between devices, exchange(): lax.all_to_all(rows, ('tod', 'map'), split_axis=0, concat_axis=0, tiled=T...  15.4 us
    pallas_call x2, Pallas kernels, read_call(): pl.pallas_call(read_kernel, out_shape=jax.ShapeDtypeStruct(offs.shape, jn...  12.6 us
    unnamed x63, local copies, waits for them, and re-layouts  10.1 us
    all_to_all x1, starting transfers between devices, exchange(): lax.all_to_all(rows, ('tod', 'map'), split_axis=0, concat_axis=0, tiled=T...  9.4 us
    ppermute x3, starting transfers between devices, extended(): lax.ppermute(tail, axis, [(i, (i + 1) % count) for i in range(ends)])  8.61 us
    dot_general x6, matrix products, owner_sum(): lax.dot_general(placement, arrived[:, j * width:(j + 1) * width], (((0,),...  7.75 us
  transfers between devices with their start and end apart: 7, of which 3 were waited for; matrix products, arithmetic and copies ran while one was open for 4% of the time, Pallas kernels for 0%

profile of v2, /device:TPU:1, one launch (start us, length us, event | category | flops | bytes accessed | tf_op | source)
XLA Modules:
  0.0 270.1 jit_solution(3987970071577972482)
XLA Ops:
  1.3 3.9 %collective-permute-start = (f32[16,128]{1,0:T(8,128)S(1)}, f32[16,128]{1,0:T(8,128)S(1)}, u32[]{:S(2)}, u32[]{:S(2)}) collective-permute-start(f32[16,128]{1,0:T(8,128)S(1)} %get-tuple-element.36), channel_id=1, source_target_pairs={{0,8},{8,16},{16,24},{24,32},{32,40},{40,48},{48,56},{56,64},{64,7... | collective-permute-start | bytes 24584 | tf_op jit(solution)/shard_map/ppermute | solution.py:23
  5.3 1.3 collective-permute-start.1
  6.6 0.8 convert_bitcast_fusion.1
  8.1 2.7 %fusion.55 = (f32[16,4096]{1,0:T(8,128)}, f32[16,4096]{1,0:T(8,128)}) fusion(s32[16,4096]{1,0:T(8,128)} %param.12, f32[16]{0:T(128)} %param.11), kind=kLoop, calls=%fused_computation.104 | loop fusion | flops 262144 | bytes 786496 | tf_op jit(solution)/shard_map/sin | solution.py:186
  10.9 5.3 %fusion.10 = f32[16,384,128]{2,0,1:T(8,128)S(1)} fusion(s32[384,128]{1,0:T(8,128)S(1)} %add_abs_fusion, bf16[1,16,129]{2,1,0:T(8,128)(2,1)S(1)} %get-tuple-element.39, bf16[1,16,129]{2,1,0:T(8,128)(2,1)S(1)} %get-tuple-element.40, bf16[1,16,129]{2,1,0:T(8,128)(2,1)S(1)} %get-tuple-element.38), kind=kOutput, calls=%fused_computation.12 | convolution fusion | flops 616648960 | bytes 3354720 | tf_op jit(solution)/shard_map/pdk,rck->pdrc/dot_general | solution.py:199
  16.3 0.8 reshape.107.slot_ref
  17.1 0.8 pad_maximum_fusion.5
  18.0 1.0 reshape.108
  19.0 2.4 fusion.8
  21.4 0.9 copy.55
  22.3 13.3 %shard_map.95 = f32[128,1536]{1,0:T(8,128)} custom-call(s32[256]{0:T(256)} %reshape.107.slot_ref, s32[16,4096]{1,0:T(8,128)} %offs_ref.9, f32[16,4096]{1,0:T(8,128)} %bitcast.160, f32[16,4096]{1,0:T(8,128)} %get-tuple-element.31.cos_ref, f32[16,4096]{1,0:T(8,128)} %get-tuple-element.30.sin_ref), custom_call_target="tpu_custom_call" | custom-call | tf_op jit(solution)/shard_map/pallas_call | solution.py:112
  35.5 1.2 maximum_bitcast_fusion
  36.7 0.9 copy.14
  37.6 28.7 %all_to_all.60 = f32[128,1,1664]{2,1,0:T(1,128)S(1)} all-to-all(f32[128,1,1664]{2,1,0:T(1,128)S(1)} %copy.14), channel_id=1, replica_groups=mesh['tod'=16,'map'=8] {'tod','map'}, dimensions={0} | all-to-all | bytes 1703936 | tf_op jit(solution)/shard_map/all_to_all | solution.py:51
  68.4 1.0 copy-done.7
  69.7 0.7 copy-done.3
  70.5 0.9 multiply_reduce_fusion.1
  71.4 1.1 gather_fusion
  74.2 21.3 %all_to_all.61 = f32[128,1,1664]{2,1,0:T(1,128)S(1)} all-to-all(f32[128,1,1664]{2,1,0:T(1,128)S(1)} %all_to_all.43), channel_id=1, replica_groups=mesh['tod'=16,'map'=8] {'tod','map'}, dimensions={0} | all-to-all | bytes 1703936 | tf_op jit(solution)/shard_map/all_to_all | solution.py:51
  95.6 0.9 copy-done.22
  96.5 1.0 reshape.111.maps_ref
  97.5 6.4 %shard_map.96 = f32[16,4096]{1,0:T(8,128)} custom-call(s32[256]{0:T(256)} %reshape.107.slot_ref, f32[256,768]{1,0:T(8,128)} %reshape.111.maps_ref, s32[16,4096]{1,0:T(8,128)} %offs_ref.9, f32[16,4096]{1,0:T(8,128)} %get-tuple-element.31.cos_ref, f32[16,4096]{1,0:T(8,128)} %get-tuple-element.30.sin_ref), custom_call_target="tpu_custom_call" | custom-call | tf_op jit(solution)/shard_map/pallas_call | solution.py:160
  104.7 2.3 collective-permute-start.2
  107.0 1.3 collective-permute-start.3
  108.3 3.1 %collective-permute-done.3 = f32[16,128]{1,0:T(8,128)S(1)} collective-permute-done((f32[16,128]{1,0:T(8,128)S(1)}, f32[16,128]{1,0:T(8,128)S(1)}, u32[]{:S(2)}, u32[]{:S(2)}) %collective-permute-start.3) | collective-permute-done | bytes 8224 | tf_op jit(solution)/shard_map/ppermute | solution.py:25
  111.4 1.7 pad_maximum_fusion.6
  113.1 1.0 reshape.112
  114.2 2.4 fusion.6
  116.6 0.8 multiply_reduce_fusion.3
  117.3 0.9 copy.54
  118.9 13.3 %shard_map.97 = f32[128,1536]{1,0:T(8,128)} custom-call(s32[256]{0:T(256)} %reshape.107.slot_ref, s32[16,4096]{1,0:T(8,128)} %offs_ref.9, f32[16,4096]{1,0:T(8,128)} %bitcast.157, f32[16,4096]{1,0:T(8,128)} %get-tuple-element.31.cos_ref, f32[16,4096]{1,0:T(8,128)} %get-tuple-element.30.sin_ref), custom_call_target="tpu_custom_call" | custom-call | tf_op jit(solution)/shard_map/pallas_call | solution.py:112
  132.1 1.2 maximum_bitcast_fusion.1
  133.3 1.8 copy.16
  135.1 9.4 %all-to-all-start.2 = ((f32[128,1,1664]{2,1,0:T(1,128)}), f32[128,1,1664]{2,1,0:T(1,128)S(1)}, u32[]{:S(2)}, u32[]{:S(2)}) async-start(f32[128,1,1664]{2,1,0:T(1,128)} %copy.16), calls=%async_computation.2 | async-start | bytes 1703936 | tf_op jit(solution)/shard_map/all_to_all | solution.py:51
  144.5 1.5 slice_reduce_fusion.3
  146.0 15.4 %all-to-all-done.2 = f32[128,1,1664]{2,1,0:T(1,128)S(1)} async-done(((f32[128,1,1664]{2,1,0:T(1,128)}), f32[128,1,1664]{2,1,0:T(1,128)S(1)}, u32[]{:S(2)}, u32[]{:S(2)}) %all-to-all-start.2) | async-done | bytes 852000 | tf_op jit(solution)/shard_map/all_to_all | solution.py:51
  161.3 1.0 copy.50
  162.3 1.6 slice_reduce_fusion.2
  163.9 1.6 fusion.38
  166.7 1.8 fusion.16
  168.8 0.7 copy-done.5
  169.5 0.9 multiply_reduce_fusion
  170.5 1.1 gather_fusion.1
  173.3 21.3 %all_to_all.62 = f32[128,1,1664]{2,1,0:T(1,128)S(1)} all-to-all(f32[128,1,1664]{2,1,0:T(1,128)S(1)} %all_to_all.49), channel_id=1, replica_groups=mesh['tod'=16,'map'=8] {'tod','map'}, dimensions={0} | all-to-all | bytes 1703936 | tf_op jit(solution)/shard_map/all_to_all | solution.py:51
  196.6 1.0 reshape.115.maps_ref
  197.6 6.2 %shard_map.98 = f32[16,4096]{1,0:T(8,128)} custom-call(s32[256]{0:T(256)} %reshape.107.slot_ref, f32[256,768]{1,0:T(8,128)} %reshape.115.maps_ref, s32[16,4096]{1,0:T(8,128)} %offs_ref.9, f32[16,4096]{1,0:T(8,128)} %get-tuple-element.31.cos_ref, f32[16,4096]{1,0:T(8,128)} %get-tuple-element.30.sin_ref), custom_call_target="tpu_custom_call" | custom-call | tf_op jit(solution)/shard_map/pallas_call | solution.py:160
  203.7 1.1 multiply_add_fusion
  204.9 2.3 collective-permute-start.4
  207.2 1.3 collective-permute-start.5
  208.5 3.1 %collective-permute-done.5 = f32[16,128]{1,0:T(8,128)S(1)} collective-permute-done((f32[16,128]{1,0:T(8,128)S(1)}, f32[16,128]{1,0:T(8,128)S(1)}, u32[]{:S(2)}, u32[]{:S(2)}) %collective-permute-start.5) | collective-permute-done | bytes 8224 | tf_op jit(solution)/shard_map/ppermute | solution.py:25
  212.4 1.0 reshape.116
  213.5 2.4 fusion.4
  215.8 0.8 multiply_reduce_fusion.2
  216.6 0.8 copy.53
  217.5 13.3 %shard_map.99 = f32[128,1536]{1,0:T(8,128)} custom-call(s32[256]{0:T(256)} %reshape.107.slot_ref, s32[16,4096]{1,0:T(8,128)} %offs_ref.9, f32[16,4096]{1,0:T(8,128)} %bitcast.158, f32[16,4096]{1,0:T(8,128)} %get-tuple-element.31.cos_ref, f32[16,4096]{1,0:T(8,128)} %get-tuple-element.30.sin_ref), custom_call_target="tpu_custom_call" | custom-call | tf_op jit(solution)/shard_map/pallas_call | solution.py:112
  231.3 1.2 maximum_bitcast_fusion.2
  232.5 0.9 copy.18
  233.4 26.0 %all_to_all.63 = f32[128,1,1664]{2,1,0:T(1,128)S(1)} all-to-all(f32[128,1,1664]{2,1,0:T(1,128)S(1)} %copy.18), channel_id=1, replica_groups=mesh['tod'=16,'map'=8] {'tod','map'}, dimensions={0} | all-to-all | bytes 1703936 | tf_op jit(solution)/shard_map/all_to_all | solution.py:51
  259.4 1.0 copy.48
  260.4 1.6 slice_reduce_fusion
  261.9 1.6 fusion.35
  264.8 1.6 fusion.14
  266.9 1.4 copy.20
  268.9 1.2 fusion.18
  (101 shorter events, 12.2 us)
Async XLA Ops:
  1.3 15.8 %collective-permute-start = (f32[16,128]{1,0:T(8,128)S(1)}, f32[16,128]{1,0:T(8,128)S(1)}, u32[]{:S(2)}, u32[]{:S(2)}) collective-permute-start(f32[16,128]{1,0:T(8,128)S(1)} %get-tuple-element.36), channel_id=1, source_target_pairs={{0,8},{8,16},{16,24},{24,32},{32,40},{40,48},{48,56},{56,64},{64,7... | collective-permute-start | bytes 24584 | tf_op jit(solution)/shard_map/ppermute | solution.py:23
  5.3 11.8 %collective-permute-start.1 = (f32[16,128]{1,0:T(8,128)S(1)}, f32[16,128]{1,0:T(8,128)S(1)}, u32[]{:S(2)}, u32[]{:S(2)}) collective-permute-start(f32[16,128]{1,0:T(8,128)S(1)} %get-tuple-element.37), channel_id=1, source_target_pairs={{8,0},{16,8},{24,16},{32,24},{40,32},{48,40},{56,48},{64,56},{72,6... | collective-permute-start | bytes 24584 | tf_op jit(solution)/shard_map/ppermute | solution.py:25
  10.9 5.5 %copy-start.26 = (s32[16,16]{1,0:T(8,128)S(1)}, s32[16,16]{1,0:T(8,128)}, u32[]{:S(2)}) copy-start(s32[16,16]{1,0:T(8,128)} %param.14) | copy-start | bytes 3076
  10.9 6.2 %copy-start.25 = (f32[16,4096]{1,0:T(8,128)S(1)}, f32[16,4096]{1,0:T(8,128)}, u32[]{:S(2)}) copy-start(f32[16,4096]{1,0:T(8,128)} %param.10) | copy-start | bytes 786436
  16.2 6.1 %copy-start = (f32[16,384,128]{2,0,1:T(8,128)}, f32[16,384,128]{2,0,1:T(8,128)S(1)}, u32[]{:S(2)}) copy-start(f32[16,384,128]{2,0,1:T(8,128)S(1)} %fusion.10) | copy-start | bytes 9437188
  67.8 1.7 copy-start.7
  69.5 1.0 copy-start.3
  69.7 1.7 copy-start.10
  69.7 1.7 copy-start.12
  69.7 1.7 copy-start.14
  95.5 0.9 copy-start.22
  97.5 16.6 %copy-start.1 = (f32[16,384,128]{2,0,1:T(8,128)S(1)}, f32[16,384,128]{2,0,1:T(8,128)}, u32[]{:S(2)}) copy-start(f32[16,384,128]{2,0,1:T(8,128)} %copy-done) | copy-start | bytes 9437188
  104.7 3.6 %collective-permute-start.2 = (f32[16,128]{1,0:T(8,128)S(1)}, f32[16,128]{1,0:T(8,128)S(1)}, u32[]{:S(2)}, u32[]{:S(2)}) collective-permute-start(f32[16,128]{1,0:T(8,128)S(1)} %get-tuple-element.34), channel_id=1, source_target_pairs={{0,8},{8,16},{16,24},{24,32},{32,40},{40,48},{48,56},{56,64},{64,7... | collective-permute-start | bytes 24584 | tf_op jit(solution)/shard_map/ppermute | solution.py:23
  107.0 4.4 %collective-permute-start.3 = (f32[16,128]{1,0:T(8,128)S(1)}, f32[16,128]{1,0:T(8,128)S(1)}, u32[]{:S(2)}, u32[]{:S(2)}) collective-permute-start(f32[16,128]{1,0:T(8,128)S(1)} %get-tuple-element.35), channel_id=1, source_target_pairs={{8,0},{16,8},{24,16},{32,24},{40,32},{48,40},{56,48},{64,56},{72,6... | collective-permute-start | bytes 24584 | tf_op jit(solution)/shard_map/ppermute | solution.py:25
  114.2 2.4 copy-start.9
  135.1 26.2 %all-to-all-start.2 = ((f32[128,1,1664]{2,1,0:T(1,128)}), f32[128,1,1664]{2,1,0:T(1,128)S(1)}, u32[]{:S(2)}, u32[]{:S(2)}) async-start(f32[128,1,1664]{2,1,0:T(1,128)} %copy.16), calls=%async_computation.2 | async-start | bytes 1703936 | tf_op jit(solution)/shard_map/all_to_all | solution.py:51
  162.3 4.4 %copy-start.4 = (f32[384,768]{1,0:T(8,128)S(1)}, f32[384,768]{1,0:T(8,128)}, u32[]{:S(2)}) copy-start(f32[384,768]{1,0:T(8,128)} %copy-done.3) | copy-start | bytes 3538948
  166.7 1.8 copy-start.8
  168.5 1.0 copy-start.5
  168.8 1.7 copy-start.16
  168.8 1.7 copy-start.18
  168.8 1.7 copy-start.20
  203.7 9.7 %copy-start.2 = (f32[16,384,128]{2,0,1:T(8,128)S(1)}, f32[16,384,128]{2,0,1:T(8,128)}, u32[]{:S(2)}) copy-start(f32[16,384,128]{2,0,1:T(8,128)} %copy-done) | copy-start | bytes 9437188
  204.9 6.8 %copy-start.23 = (f32[16,4096]{1,0:T(8,128)}, f32[16,4096]{1,0:T(8,128)S(1)}, u32[]{:S(2)}) copy-start(f32[16,4096]{1,0:T(8,128)S(1)} %multiply_add_fusion) | copy-start | bytes 786436
  204.9 3.7 %collective-permute-start.4 = (f32[16,128]{1,0:T(8,128)S(1)}, f32[16,128]{1,0:T(8,128)S(1)}, u32[]{:S(2)}, u32[]{:S(2)}) collective-permute-start(f32[16,128]{1,0:T(8,128)S(1)} %get-tuple-element.32), channel_id=1, source_target_pairs={{0,8},{8,16},{16,24},{24,32},{32,40},{40,48},{48,56},{56,64},{64,7... | collective-permute-start | bytes 24584 | tf_op jit(solution)/shard_map/ppermute | solution.py:23
  207.2 4.4 %collective-permute-start.5 = (f32[16,128]{1,0:T(8,128)S(1)}, f32[16,128]{1,0:T(8,128)S(1)}, u32[]{:S(2)}, u32[]{:S(2)}) collective-permute-start(f32[16,128]{1,0:T(8,128)S(1)} %get-tuple-element.33), channel_id=1, source_target_pairs={{8,0},{16,8},{24,16},{32,24},{40,32},{48,40},{56,48},{64,56},{72,6... | collective-permute-start | bytes 24584 | tf_op jit(solution)/shard_map/ppermute | solution.py:25
  213.5 2.4 copy-start.24
  260.4 4.5 %copy-start.6 = (f32[384,768]{1,0:T(8,128)S(1)}, f32[384,768]{1,0:T(8,128)}, u32[]{:S(2)}) copy-start(f32[384,768]{1,0:T(8,128)} %copy-done.5) | copy-start | bytes 3538948
  266.8 1.4 copy-start.11
  266.8 1.4 copy-start.13
  266.8 1.4 copy-start.15
  266.9 1.4 copy-start.17
  266.9 1.8 copy-start.19
  266.9 2.0 copy-start.21

commit v3 on v1

--- a/solution.py
+++ b/solution.py
@@ -236,10 +236,13 @@
         return owner_sum(arrived, owner_flat, owner_index), total
 
     def projection(field, partial):
-        outgoing = jnp.where(
-            (owner_flat >= 0)[:, None],
-            jnp.take(field, owner_index, axis=0),
-            0.0,
+        outgoing = jnp.dot(
+            (owner_flat[:, None] == jnp.arange(tiles_dev, dtype=jnp.int32)[None, :]).astype(
+                jnp.float32
+            ),
+            field,
+            precision=highest,
+            preferred_element_type=jnp.float32,
         )
         touched, total = exchange(outgoing.reshape(shards, slot_count * 3 * tile_pix), partial)
         stream = read_call(

time: 264 us -> 288 us (1.091)
  local copies, waits for them, and re-layouts: 26.6 us -> 40.9 us
  matrix products: 14.2 us -> 20.1 us
  other arithmetic: 23.8 us -> 27.6 us
    reshape x2, local copies, waits for them, and re-layouts: 0.44 us -> 4.48 us  [projection(): outgoing.reshape(shards, slot_count * 3 * tile_pix)]
    dot_general x0 -> x2, matrix products: none -> 3.04 us  [projection(): jnp.dot((owner_flat[:, None] == jnp.arange(tiles_dev, dtype=jnp.int32)[No...]
    unnamed x63 -> x49, local copies, waits for them, and re-layouts: 8.36 us -> 8.55 us
  transfers between devices with their start and end apart: 7 -> 7, of which waited for: 3 -> 3; matrix products, arithmetic and copies ran while one was open for 5% -> 4% of each run, Pallas kernels for 0% -> 0%
where the time goes in v3:
time: 288 us; the launch traced here: 287 us
  blocking collectives  97.3 us (34%)
  Pallas kernels  52.1 us (18%)
  local copies, waits for them, and re-layouts  40.9 us (14%)
  other arithmetic  27.6 us (10%)
  starting transfers between devices  22.5 us (8%)
  waiting for transfers between devices  21 us (7%)
  matrix products  20.1 us (7%)
  between operations  5.15 us (2%)
    all_to_all x4, blocking collectives, exchange(): lax.all_to_all(rows, ('tod', 'map'), split_axis=0, concat_axis=0, tiled=T...  97.3 us
    pallas_call x3, Pallas kernels, bin_call(): pl.pallas_call(functools.partial(bin_kernel, slots=slots), out_shape=jax....  39.8 us
    all_to_all x1, waiting for transfers between devices, exchange(): lax.all_to_all(rows, ('tod', 'map'), split_axis=0, concat_axis=0, tiled=T...  15 us
    pallas_call x2, Pallas kernels, read_call(): pl.pallas_call(read_kernel, out_shape=jax.ShapeDtypeStruct(offs.shape, jn...  12.3 us
    all_to_all x1, starting transfers between devices, exchange(): lax.all_to_all(rows, ('tod', 'map'), split_axis=0, concat_axis=0, tiled=T...  9.8 us
    ppermute x3, starting transfers between devices, extended(): lax.ppermute(tail, axis, [(i, (i + 1) % count) for i in range(ends)])  8.61 us
    unnamed x49, local copies, waits for them, and re-layouts  8.55 us
    dot_general x3, matrix products, weigh(): jnp.einsum('dbj,dji->dbi', stacked, toeplitz, precision=highest, preferre...  7.09 us
  transfers between devices with their start and end apart: 7, of which 3 were waited for; matrix products, arithmetic and copies ran while one was open for 4% of the time, Pallas kernels for 0%

profile of v3, /device:TPU:1, one launch (start us, length us, event | category | flops | bytes accessed | tf_op | source)
XLA Modules:
  0.0 286.6 jit_solution(11553122801496724177)
XLA Ops:
  1.3 3.9 %collective-permute-start = (f32[16,128]{1,0:T(8,128)S(1)}, f32[16,128]{1,0:T(8,128)S(1)}, u32[]{:S(2)}, u32[]{:S(2)}) collective-permute-start(f32[16,128]{1,0:T(8,128)S(1)} %get-tuple-element.29), channel_id=1, source_target_pairs={{0,8},{8,16},{16,24},{24,32},{32,40},{40,48},{48,56},{56,64},{64,7... | collective-permute-start | bytes 24584 | tf_op jit(solution)/shard_map/ppermute | solution.py:23
  5.3 1.3 collective-permute-start.1
  8.1 2.7 fusion.47
  10.9 5.3 %fusion.10 = f32[16,384,128]{2,0,1:T(8,128)S(1)} fusion(s32[384,128]{1,0:T(8,128)S(1)} %add_abs_fusion, bf16[1,16,129]{2,1,0:T(8,128)(2,1)S(1)} %get-tuple-element.32, bf16[1,16,129]{2,1,0:T(8,128)(2,1)S(1)} %get-tuple-element.33, bf16[1,16,129]{2,1,0:T(8,128)(2,1)S(1)} %get-tuple-element.31), kind=kOutput, calls=%fused_computation.10 | convolution fusion | flops 616648960 | bytes 3354720 | tf_op jit(solution)/shard_map/pdk,rck->pdrc/dot_general | solution.py:199
  17.7 1.0 reshape.102
  18.7 2.4 fusion.8
  22.0 13.3 %shard_map.95 = f32[128,1536]{1,0:T(8,128)} custom-call(s32[256]{0:T(256)} %reshape.101.slot_ref, s32[16,4096]{1,0:T(8,128)} %offs_ref.9, f32[16,4096]{1,0:T(8,128)} %bitcast.164, f32[16,4096]{1,0:T(8,128)} %get-tuple-element.24.cos_ref, f32[16,4096]{1,0:T(8,128)} %get-tuple-element.23.sin_ref), custom_call_target="tpu_custom_call" | custom-call | tf_op jit(solution)/shard_map/pallas_call | solution.py:112
  35.2 1.2 maximum_bitcast_fusion
  36.4 0.9 copy.14
  37.3 28.7 %all_to_all.60 = f32[128,1,1664]{2,1,0:T(1,128)S(1)} all-to-all(f32[128,1,1664]{2,1,0:T(1,128)S(1)} %copy.14), channel_id=1, replica_groups=mesh['tod'=16,'map'=8] {'tod','map'}, dimensions={0} | all-to-all | bytes 1703936 | tf_op jit(solution)/shard_map/all_to_all | solution.py:51
  66.2 1.0 slice.172
  67.3 2.1 reshape.104
  69.4 1.7 fusion.46
  71.2 2.2 fusion.42
  73.4 0.9 multiply_reduce_fusion.1
  74.4 1.5 fusion.18
  76.4 2.2 reshape.105
  78.7 1.2 pad_maximum_fusion.3
  80.5 21.3 %all_to_all.61 = f32[128,1,1664]{2,1,0:T(1,128)S(1)} all-to-all(f32[128,1,1664]{2,1,0:T(1,128)S(1)} %all_to_all.43), channel_id=1, replica_groups=mesh['tod'=16,'map'=8] {'tod','map'}, dimensions={0} | all-to-all | bytes 1703936 | tf_op jit(solution)/shard_map/all_to_all | solution.py:51
  101.8 0.9 copy-done.15
  102.7 1.0 slice.177
  103.7 2.1 reshape.106.maps_ref
  105.8 6.1 %shard_map.96 = f32[16,4096]{1,0:T(8,128)} custom-call(s32[256]{0:T(256)} %reshape.101.slot_ref, f32[256,768]{1,0:T(8,128)} %reshape.106.maps_ref, s32[16,4096]{1,0:T(8,128)} %offs_ref.9, f32[16,4096]{1,0:T(8,128)} %get-tuple-element.24.cos_ref, f32[16,4096]{1,0:T(8,128)} %get-tuple-element.23.sin_ref), custom_call_target="tpu_custom_call" | custom-call | tf_op jit(solution)/shard_map/pallas_call | solution.py:160
  112.7 2.3 collective-permute-start.2
  115.0 1.3 collective-permute-start.3
  116.3 3.1 %collective-permute-done.3 = f32[16,128]{1,0:T(8,128)S(1)} collective-permute-done((f32[16,128]{1,0:T(8,128)S(1)}, f32[16,128]{1,0:T(8,128)S(1)}, u32[]{:S(2)}, u32[]{:S(2)}) %collective-permute-start.3) | collective-permute-done | bytes 8224 | tf_op jit(solution)/shard_map/ppermute | solution.py:25
  119.4 1.7 pad_maximum_fusion.8
  121.1 1.7 reshape.107
  122.8 1.3 fusion.75
  124.1 2.4 fusion.6
  127.2 0.9 copy.54
  128.8 13.3 %shard_map.97 = f32[128,1536]{1,0:T(8,128)} custom-call(s32[256]{0:T(256)} %reshape.101.slot_ref, s32[16,4096]{1,0:T(8,128)} %offs_ref.9, f32[16,4096]{1,0:T(8,128)} %bitcast.161, f32[16,4096]{1,0:T(8,128)} %get-tuple-element.24.cos_ref, f32[16,4096]{1,0:T(8,128)} %get-tuple-element.23.sin_ref), custom_call_target="tpu_custom_call" | custom-call | tf_op jit(solution)/shard_map/pallas_call | solution.py:112
  142.0 1.2 maximum_bitcast_fusion.1
  143.2 1.8 copy.16
  145.0 9.8 %all-to-all-start.2 = ((f32[128,1,1664]{2,1,0:T(1,128)}), f32[128,1,1664]{2,1,0:T(1,128)}, u32[]{:S(2)}, u32[]{:S(2)}) async-start(f32[128,1,1664]{2,1,0:T(1,128)} %copy.16), calls=%async_computation.2 | async-start | bytes 1703936 | tf_op jit(solution)/shard_map/all_to_all | solution.py:51
  154.8 1.5 slice_reduce_fusion.3
  156.3 15.0 %all-to-all-done.2 = f32[128,1,1664]{2,1,0:T(1,128)} async-done(((f32[128,1,1664]{2,1,0:T(1,128)}), f32[128,1,1664]{2,1,0:T(1,128)}, u32[]{:S(2)}, u32[]{:S(2)}) %all-to-all-start.2) | async-done | bytes 852000 | tf_op jit(solution)/shard_map/all_to_all | solution.py:51
  171.3 1.2 copy.50
  173.2 1.0 slice.184
  174.1 2.1 reshape.109
  177.6 2.3 fusion.13
  180.9 0.9 multiply_reduce_fusion
  181.8 1.5 fusion.17
  183.9 2.3 reshape.110
  186.2 1.2 pad_maximum_fusion.4
  188.0 21.3 %all_to_all.62 = f32[128,1,1664]{2,1,0:T(1,128)S(1)} all-to-all(f32[128,1,1664]{2,1,0:T(1,128)S(1)} %all_to_all.49), channel_id=1, replica_groups=mesh['tod'=16,'map'=8] {'tod','map'}, dimensions={0} | all-to-all | bytes 1703936 | tf_op jit(solution)/shard_map/all_to_all | solution.py:51
  210.0 1.0 slice.189
  212.2 2.1 reshape.111.maps_ref
  214.3 6.2 %shard_map.98 = f32[16,4096]{1,0:T(8,128)} custom-call(s32[256]{0:T(256)} %reshape.101.slot_ref, f32[256,768]{1,0:T(8,128)} %reshape.111.maps_ref, s32[16,4096]{1,0:T(8,128)} %offs_ref.9, f32[16,4096]{1,0:T(8,128)} %get-tuple-element.24.cos_ref, f32[16,4096]{1,0:T(8,128)} %get-tuple-element.23.sin_ref), custom_call_target="tpu_custom_call" | custom-call | tf_op jit(solution)/shard_map/pallas_call | solution.py:160
  220.5 1.1 multiply_add_fusion
  221.6 2.3 collective-permute-start.4
  223.9 1.5 collective-permute-start.5
  225.5 2.9 collective-permute-done.5
  229.1 1.7 reshape.112
  230.8 1.3 fusion.74
  232.1 2.4 fusion.4
  235.3 0.9 copy.53
  236.1 13.3 %shard_map.99 = f32[128,1536]{1,0:T(8,128)} custom-call(s32[256]{0:T(256)} %reshape.101.slot_ref, s32[16,4096]{1,0:T(8,128)} %offs_ref.9, f32[16,4096]{1,0:T(8,128)} %bitcast.162, f32[16,4096]{1,0:T(8,128)} %get-tuple-element.24.cos_ref, f32[16,4096]{1,0:T(8,128)} %get-tuple-element.23.sin_ref), custom_call_target="tpu_custom_call" | custom-call | tf_op jit(solution)/shard_map/pallas_call | solution.py:112
  250.1 1.2 maximum_bitcast_fusion.2
  251.3 0.9 copy.18
  252.2 26.0 %all_to_all.63 = f32[128,1,1664]{2,1,0:T(1,128)S(1)} all-to-all(f32[128,1,1664]{2,1,0:T(1,128)S(1)} %copy.18), channel_id=1, replica_groups=mesh['tod'=16,'map'=8] {'tod','map'}, dimensions={0} | all-to-all | bytes 1703936 | tf_op jit(solution)/shard_map/all_to_all | solution.py:51
  281.1 1.4 copy.19
  282.5 2.8 copy.20
  285.4 1.2 fusion.16
  (81 shorter events, 15.5 us)
Async XLA Ops:
  1.3 15.6 %collective-permute-start = (f32[16,128]{1,0:T(8,128)S(1)}, f32[16,128]{1,0:T(8,128)S(1)}, u32[]{:S(2)}, u32[]{:S(2)}) collective-permute-start(f32[16,128]{1,0:T(8,128)S(1)} %get-tuple-element.29), channel_id=1, source_target_pairs={{0,8},{8,16},{16,24},{24,32},{32,40},{40,48},{48,56},{56,64},{64,7... | collective-permute-start | bytes 24584 | tf_op jit(solution)/shard_map/ppermute | solution.py:23
  5.3 11.6 %collective-permute-start.1 = (f32[16,128]{1,0:T(8,128)S(1)}, f32[16,128]{1,0:T(8,128)S(1)}, u32[]{:S(2)}, u32[]{:S(2)}) collective-permute-start(f32[16,128]{1,0:T(8,128)S(1)} %get-tuple-element.30), channel_id=1, source_target_pairs={{8,0},{16,8},{24,16},{32,24},{40,32},{48,40},{56,48},{64,56},{72,6... | collective-permute-start | bytes 24584 | tf_op jit(solution)/shard_map/ppermute | solution.py:25
  10.9 5.5 %copy-start.19 = (s32[16,16]{1,0:T(8,128)S(1)}, s32[16,16]{1,0:T(8,128)}, u32[]{:S(2)}) copy-start(s32[16,16]{1,0:T(8,128)} %param.12) | copy-start | bytes 3076
  10.9 6.1 %copy-start.18 = (f32[16,4096]{1,0:T(8,128)S(1)}, f32[16,4096]{1,0:T(8,128)}, u32[]{:S(2)}) copy-start(f32[16,4096]{1,0:T(8,128)} %param.8) | copy-start | bytes 786436
  71.2 2.3 copy-start.2
  73.4 0.9 copy-start.4
  73.4 0.9 copy-start.6
  101.8 0.9 copy-start.15
  112.7 3.6 %collective-permute-start.2 = (f32[16,128]{1,0:T(8,128)S(1)}, f32[16,128]{1,0:T(8,128)S(1)}, u32[]{:S(2)}, u32[]{:S(2)}) collective-permute-start(f32[16,128]{1,0:T(8,128)S(1)} %get-tuple-element.27), channel_id=1, source_target_pairs={{0,8},{8,16},{16,24},{24,32},{32,40},{40,48},{48,56},{56,64},{64,7... | collective-permute-start | bytes 24584 | tf_op jit(solution)/shard_map/ppermute | solution.py:23
  115.0 4.4 %collective-permute-start.3 = (f32[16,128]{1,0:T(8,128)S(1)}, f32[16,128]{1,0:T(8,128)S(1)}, u32[]{:S(2)}, u32[]{:S(2)}) collective-permute-start(f32[16,128]{1,0:T(8,128)S(1)} %get-tuple-element.28), channel_id=1, source_target_pairs={{8,0},{16,8},{24,16},{32,24},{40,32},{48,40},{56,48},{64,56},{72,6... | collective-permute-start | bytes 24584 | tf_op jit(solution)/shard_map/ppermute | solution.py:25
  124.1 2.4 copy-start.14
  145.0 26.3 %all-to-all-start.2 = ((f32[128,1,1664]{2,1,0:T(1,128)}), f32[128,1,1664]{2,1,0:T(1,128)}, u32[]{:S(2)}, u32[]{:S(2)}) async-start(f32[128,1,1664]{2,1,0:T(1,128)} %copy.16), calls=%async_computation.2 | async-start | bytes 1703936 | tf_op jit(solution)/shard_map/all_to_all | solution.py:51
  177.5 2.3 copy-start.3
  179.8 1.0 copy-start
  180.1 1.7 copy-start.8
  180.1 1.7 copy-start.10
  180.1 1.7 copy-start.12
  221.5 6.8 %copy-start.16 = (f32[16,4096]{1,0:T(8,128)}, f32[16,4096]{1,0:T(8,128)S(1)}, u32[]{:S(2)}) copy-start(f32[16,4096]{1,0:T(8,128)S(1)} %multiply_add_fusion) | copy-start | bytes 786436
  221.6 3.9 %collective-permute-start.4 = (f32[16,128]{1,0:T(8,128)S(1)}, f32[16,128]{1,0:T(8,128)S(1)}, u32[]{:S(2)}, u32[]{:S(2)}) collective-permute-start(f32[16,128]{1,0:T(8,128)S(1)} %get-tuple-element.25), channel_id=1, source_target_pairs={{0,8},{8,16},{16,24},{24,32},{32,40},{40,48},{48,56},{56,64},{64,7... | collective-permute-start | bytes 24584 | tf_op jit(solution)/shard_map/ppermute | solution.py:23
  223.9 4.4 %collective-permute-start.5 = (f32[16,128]{1,0:T(8,128)S(1)}, f32[16,128]{1,0:T(8,128)S(1)}, u32[]{:S(2)}, u32[]{:S(2)}) collective-permute-start(f32[16,128]{1,0:T(8,128)S(1)} %get-tuple-element.26), channel_id=1, source_target_pairs={{8,0},{16,8},{24,16},{32,24},{40,32},{48,40},{56,48},{64,56},{72,6... | collective-permute-start | bytes 24584 | tf_op jit(solution)/shard_map/ppermute | solution.py:25
  232.1 2.4 copy-start.17
  279.0 1.5 copy-start.1
  282.5 2.8 copy-start.5
  282.5 2.8 copy-start.7
  282.5 2.8 copy-start.9
  282.5 2.8 copy-start.11
  282.5 2.8 copy-start.13

commit v4 on v1

--- a/solution.py
+++ b/solution.py
@@ -121,22 +121,25 @@
     )(slot_ids, offs, y, cos, sin)
 
 
+READ_GROUP = 16
+
+
 def read_kernel(slot_ref, maps_ref, offs_ref, cos_ref, sin_ref, out_ref):
     lanes = 128
     dets, samples = offs_ref.shape
     blocks = slot_ref.shape[0] // dets
     tile = maps_ref.shape[1] // 3
 
-    for first in range(0, dets, GROUP):
+    for first in range(0, dets, READ_GROUP):
         def body(blk, carry):
             rows = jnp.concatenate(
-                [maps_ref[pl.ds(slot_ref[(first + i) * blocks + blk], 1), :] for i in range(GROUP)],
+                [maps_ref[pl.ds(slot_ref[(first + i) * blocks + blk], 1), :] for i in range(READ_GROUP)],
                 axis=0,
             )
             for j in range(tile // lanes):
                 start = pl.multiple_of(blk * tile + j * lanes, lanes)
                 cols = pl.ds(start, lanes)
-                idx = offs_ref[first : first + GROUP, cols]
+                idx = offs_ref[first : first + READ_GROUP, cols]
                 low = idx % lanes
                 upper = idx >= lanes
                 picked = []
@@ -148,9 +151,9 @@
                         rows[:, s * tile + lanes : (s + 1) * tile], low, axis=1, mode="promise_in_bounds"
                     )
                     picked.append(jnp.where(upper, b, a))
-                c = cos_ref[first : first + GROUP, cols]
-                sn = sin_ref[first : first + GROUP, cols]
-                out_ref[first : first + GROUP, cols] = picked[0] + c * picked[1] + sn * picked[2]
+                c = cos_ref[first : first + READ_GROUP, cols]
+                sn = sin_ref[first : first + READ_GROUP, cols]
+                out_ref[first : first + READ_GROUP, cols] = picked[0] + c * picked[1] + sn * picked[2]
             return carry
 
         lax.fori_loop(0, blocks, body, 0)

time: 264 us -> 262 us (level)
  no operation moved by 1% of the time
where the time goes in v4:
time: 262 us; the launch traced here: 261 us
  blocking collectives  97.3 us (37%)
  Pallas kernels  50.5 us (19%)
  local copies, waits for them, and re-layouts  26.6 us (10%)
  other arithmetic  23.8 us (9%)
  starting transfers between devices  22.1 us (8%)
  waiting for transfers between devices  21.3 us (8%)
  matrix products  14.2 us (5%)
  between operations  5.45 us (2%)
    all_to_all x4, blocking collectives, exchange(): lax.all_to_all(rows, ('tod', 'map'), split_axis=0, concat_axis=0, tiled=T...  97.3 us
    pallas_call x3, Pallas kernels, bin_call(): pl.pallas_call(functools.partial(bin_kernel, slots=slots), out_shape=jax....  39.8 us
    all_to_all x1, waiting for transfers between devices, exchange(): lax.all_to_all(rows, ('tod', 'map'), split_axis=0, concat_axis=0, tiled=T...  15.3 us
    pallas_call x2, Pallas kernels, read_call(): pl.pallas_call(read_kernel, out_shape=jax.ShapeDtypeStruct(offs.shape, jn...  10.7 us
    all_to_all x1, starting transfers between devices, exchange(): lax.all_to_all(rows, ('tod', 'map'), split_axis=0, concat_axis=0, tiled=T...  9.39 us
    ppermute x3, starting transfers between devices, extended(): lax.ppermute(tail, axis, [(i, (i + 1) % count) for i in range(ends)])  8.61 us
    unnamed x63, local copies, waits for them, and re-layouts  8.36 us
    dot_general x3, matrix products, weigh(): jnp.einsum('dbj,dji->dbi', stacked, toeplitz, precision=highest, preferre...  7.1 us
  transfers between devices with their start and end apart: 7, of which 3 were waited for; matrix products, arithmetic and copies ran while one was open for 5% of the time, Pallas kernels for 0%

profile of v4, /device:TPU:1, one launch (start us, length us, event | category | flops | bytes accessed | tf_op | source)
XLA Modules:
  0.0 261.2 jit_solution(8563962236934342899)
XLA Ops:
  0.6 0.7 fusion.73
  1.3 3.9 %collective-permute-start = (f32[16,128]{1,0:T(8,128)S(1)}, f32[16,128]{1,0:T(8,128)S(1)}, u32[]{:S(2)}, u32[]{:S(2)}) collective-permute-start(f32[16,128]{1,0:T(8,128)S(1)} %get-tuple-element.34), channel_id=1, source_target_pairs={{0,8},{8,16},{16,24},{24,32},{32,40},{40,48},{48,56},{56,64},{64,7... | collective-permute-start | bytes 24584 | tf_op jit(solution)/shard_map/ppermute | solution.py:23
  5.3 1.3 collective-permute-start.1
  6.6 0.8 convert_bitcast_fusion.1
  7.4 0.7 fusion.58
  8.1 2.7 %fusion.45 = (f32[16,4096]{1,0:T(8,128)}, f32[16,4096]{1,0:T(8,128)}) fusion(s32[16,4096]{1,0:T(8,128)} %param.12, f32[16]{0:T(128)} %param.11), kind=kLoop, calls=%fused_computation.94 | loop fusion | flops 262144 | bytes 786496 | tf_op jit(solution)/shard_map/sin | solution.py:189
  10.9 5.3 %fusion.10 = f32[16,384,128]{2,0,1:T(8,128)S(1)} fusion(s32[384,128]{1,0:T(8,128)S(1)} %add_abs_fusion, bf16[1,16,129]{2,1,0:T(8,128)(2,1)S(1)} %get-tuple-element.37, bf16[1,16,129]{2,1,0:T(8,128)(2,1)S(1)} %get-tuple-element.38, bf16[1,16,129]{2,1,0:T(8,128)(2,1)S(1)} %get-tuple-element.36), kind=kOutput, calls=%fused_computation.12 | convolution fusion | flops 616648960 | bytes 3354720 | tf_op jit(solution)/shard_map/pdk,rck->pdrc/dot_general | solution.py:202
  16.3 0.8 reshape.114.slot_ref
  17.2 0.8 pad_maximum_fusion.5
  18.0 1.0 reshape.115
  19.1 2.4 fusion.8
  21.4 0.9 copy.55
  22.3 13.3 %shard_map.95 = f32[128,1536]{1,0:T(8,128)} custom-call(s32[256]{0:T(256)} %reshape.114.slot_ref, s32[16,4096]{1,0:T(8,128)} %offs_ref.9, f32[16,4096]{1,0:T(8,128)} %bitcast.164, f32[16,4096]{1,0:T(8,128)} %get-tuple-element.29.cos_ref, f32[16,4096]{1,0:T(8,128)} %get-tuple-element.28.sin_ref), custom_call_target="tpu_custom_call" | custom-call | tf_op jit(solution)/shard_map/pallas_call | solution.py:112
  35.5 1.2 maximum_bitcast_fusion
  36.7 0.9 copy.14
  37.6 28.7 %all_to_all.60 = f32[128,1,1664]{2,1,0:T(1,128)S(1)} all-to-all(f32[128,1,1664]{2,1,0:T(1,128)S(1)} %copy.14), channel_id=1, replica_groups=mesh['tod'=16,'map'=8] {'tod','map'}, dimensions={0} | all-to-all | bytes 1703936 | tf_op jit(solution)/shard_map/all_to_all | solution.py:51
  66.5 1.0 slice.176
  67.6 1.4 reshape.118
  70.0 0.7 copy-done.5
  70.7 0.9 multiply_reduce_fusion.1
  71.6 1.1 gather_fusion
  73.1 0.7 fusion.63
  74.4 21.3 %all_to_all.61 = f32[128,1,1664]{2,1,0:T(1,128)S(1)} all-to-all(f32[128,1,1664]{2,1,0:T(1,128)S(1)} %all_to_all.43), channel_id=1, replica_groups=mesh['tod'=16,'map'=8] {'tod','map'}, dimensions={0} | all-to-all | bytes 1703936 | tf_op jit(solution)/shard_map/all_to_all | solution.py:51
  95.8 0.9 copy-done.22
  96.8 1.0 reshape.120.maps_ref
  97.8 5.5 %shard_map.96 = f32[16,4096]{1,0:T(8,128)} custom-call(s32[256]{0:T(256)} %reshape.114.slot_ref, f32[256,768]{1,0:T(8,128)} %reshape.120.maps_ref, s32[16,4096]{1,0:T(8,128)} %offs_ref.9, f32[16,4096]{1,0:T(8,128)} %get-tuple-element.29.cos_ref, f32[16,4096]{1,0:T(8,128)} %get-tuple-element.28.sin_ref), custom_call_target="tpu_custom_call" | custom-call | tf_op jit(solution)/shard_map/pallas_call | solution.py:163
  103.3 0.7 fusion.72
  104.0 2.3 collective-permute-start.2
  106.3 1.3 collective-permute-start.3
  107.6 3.1 %collective-permute-done.3 = f32[16,128]{1,0:T(8,128)S(1)} collective-permute-done((f32[16,128]{1,0:T(8,128)S(1)}, f32[16,128]{1,0:T(8,128)S(1)}, u32[]{:S(2)}, u32[]{:S(2)}) %collective-permute-start.3) | collective-permute-done | bytes 8224 | tf_op jit(solution)/shard_map/ppermute | solution.py:25
  110.7 1.7 pad_maximum_fusion.6
  112.4 1.0 reshape.121
  113.5 2.4 fusion.6
  115.9 0.8 multiply_reduce_fusion.3
  116.6 0.9 copy.54
  118.2 13.3 %shard_map.97 = f32[128,1536]{1,0:T(8,128)} custom-call(s32[256]{0:T(256)} %reshape.114.slot_ref, s32[16,4096]{1,0:T(8,128)} %offs_ref.9, f32[16,4096]{1,0:T(8,128)} %bitcast.161, f32[16,4096]{1,0:T(8,128)} %get-tuple-element.29.cos_ref, f32[16,4096]{1,0:T(8,128)} %get-tuple-element.28.sin_ref), custom_call_target="tpu_custom_call" | custom-call | tf_op jit(solution)/shard_map/pallas_call | solution.py:112
  131.5 1.2 maximum_bitcast_fusion.1
  132.6 1.8 copy.16
  134.4 9.4 %all-to-all-start.2 = ((f32[128,1,1664]{2,1,0:T(1,128)}), f32[128,1,1664]{2,1,0:T(1,128)S(1)}, u32[]{:S(2)}, u32[]{:S(2)}) async-start(f32[128,1,1664]{2,1,0:T(1,128)} %copy.16), calls=%async_computation.2 | async-start | bytes 1703936 | tf_op jit(solution)/shard_map/all_to_all | solution.py:51
  143.8 1.5 slice_reduce_fusion.3
  145.3 15.3 %all-to-all-done.2 = f32[128,1,1664]{2,1,0:T(1,128)S(1)} async-done(((f32[128,1,1664]{2,1,0:T(1,128)}), f32[128,1,1664]{2,1,0:T(1,128)S(1)}, u32[]{:S(2)}, u32[]{:S(2)}) %all-to-all-start.2) | async-done | bytes 852000 | tf_op jit(solution)/shard_map/all_to_all | solution.py:51
  163.6 1.0 copy-done.8
  164.9 0.7 copy-done.3
  165.6 0.9 multiply_reduce_fusion
  166.6 1.1 gather_fusion.1
  168.0 0.7 fusion.61
  169.4 21.3 %all_to_all.62 = f32[128,1,1664]{2,1,0:T(1,128)S(1)} all-to-all(f32[128,1,1664]{2,1,0:T(1,128)S(1)} %all_to_all.49), channel_id=1, replica_groups=mesh['tod'=16,'map'=8] {'tod','map'}, dimensions={0} | all-to-all | bytes 1703936 | tf_op jit(solution)/shard_map/all_to_all | solution.py:51
  192.7 1.0 reshape.125.maps_ref
  193.7 5.2 %shard_map.98 = f32[16,4096]{1,0:T(8,128)} custom-call(s32[256]{0:T(256)} %reshape.114.slot_ref, f32[256,768]{1,0:T(8,128)} %reshape.125.maps_ref, s32[16,4096]{1,0:T(8,128)} %offs_ref.9, f32[16,4096]{1,0:T(8,128)} %get-tuple-element.29.cos_ref, f32[16,4096]{1,0:T(8,128)} %get-tuple-element.28.sin_ref), custom_call_target="tpu_custom_call" | custom-call | tf_op jit(solution)/shard_map/pallas_call | solution.py:163
  198.9 1.1 multiply_add_fusion
  200.1 2.3 collective-permute-start.4
  202.4 1.5 collective-permute-start.5
  204.0 2.9 %collective-permute-done.5 = f32[16,128]{1,0:T(8,128)S(1)} collective-permute-done((f32[16,128]{1,0:T(8,128)S(1)}, f32[16,128]{1,0:T(8,128)S(1)}, u32[]{:S(2)}, u32[]{:S(2)}) %collective-permute-start.5) | collective-permute-done | bytes 8224 | tf_op jit(solution)/shard_map/ppermute | solution.py:25
  206.8 0.7 pad_maximum_fusion.7
  207.6 1.0 reshape.126
  208.7 2.4 fusion.4
  211.0 0.8 multiply_reduce_fusion.2
  211.8 0.9 copy.53
  212.7 13.3 %shard_map.99 = f32[128,1536]{1,0:T(8,128)} custom-call(s32[256]{0:T(256)} %reshape.114.slot_ref, s32[16,4096]{1,0:T(8,128)} %offs_ref.9, f32[16,4096]{1,0:T(8,128)} %bitcast.162, f32[16,4096]{1,0:T(8,128)} %get-tuple-element.29.cos_ref, f32[16,4096]{1,0:T(8,128)} %get-tuple-element.28.sin_ref), custom_call_target="tpu_custom_call" | custom-call | tf_op jit(solution)/shard_map/pallas_call | solution.py:112
  226.6 1.2 maximum_bitcast_fusion.2
  227.8 0.9 copy.18
  228.7 26.0 %all_to_all.63 = f32[128,1,1664]{2,1,0:T(1,128)S(1)} all-to-all(f32[128,1,1664]{2,1,0:T(1,128)S(1)} %copy.18), channel_id=1, replica_groups=mesh['tod'=16,'map'=8] {'tod','map'}, dimensions={0} | all-to-all | bytes 1703936 | tf_op jit(solution)/shard_map/all_to_all | solution.py:51
  258.0 1.4 copy.20
  260.0 1.2 fusion.16
  (100 shorter events, 9.9 us)
Async XLA Ops:
  1.3 15.8 %collective-permute-start = (f32[16,128]{1,0:T(8,128)S(1)}, f32[16,128]{1,0:T(8,128)S(1)}, u32[]{:S(2)}, u32[]{:S(2)}) collective-permute-start(f32[16,128]{1,0:T(8,128)S(1)} %get-tuple-element.34), channel_id=1, source_target_pairs={{0,8},{8,16},{16,24},{24,32},{32,40},{40,48},{48,56},{56,64},{64,7... | collective-permute-start | bytes 24584 | tf_op jit(solution)/shard_map/ppermute | solution.py:23
  5.3 11.9 %collective-permute-start.1 = (f32[16,128]{1,0:T(8,128)S(1)}, f32[16,128]{1,0:T(8,128)S(1)}, u32[]{:S(2)}, u32[]{:S(2)}) collective-permute-start(f32[16,128]{1,0:T(8,128)S(1)} %get-tuple-element.35), channel_id=1, source_target_pairs={{8,0},{16,8},{24,16},{32,24},{40,32},{48,40},{56,48},{64,56},{72,6... | collective-permute-start | bytes 24584 | tf_op jit(solution)/shard_map/ppermute | solution.py:25
  10.9 5.5 %copy-start.26 = (s32[16,16]{1,0:T(8,128)S(1)}, s32[16,16]{1,0:T(8,128)}, u32[]{:S(2)}) copy-start(s32[16,16]{1,0:T(8,128)} %param.14) | copy-start | bytes 3076
  10.9 6.3 %copy-start.25 = (f32[16,4096]{1,0:T(8,128)S(1)}, f32[16,4096]{1,0:T(8,128)}, u32[]{:S(2)}) copy-start(f32[16,4096]{1,0:T(8,128)} %param.10) | copy-start | bytes 786436
  16.2 6.1 %copy-start = (f32[16,384,128]{2,0,1:T(8,128)}, f32[16,384,128]{2,0,1:T(8,128)S(1)}, u32[]{:S(2)}) copy-start(f32[16,384,128]{2,0,1:T(8,128)S(1)} %fusion.10) | copy-start | bytes 9437188
  67.6 2.0 copy-start.7
  69.7 1.0 copy-start.5
  69.9 1.7 copy-start.10
  69.9 1.7 copy-start.12
  70.0 1.7 copy-start.14
  95.8 0.9 copy-start.22
  97.8 15.7 %copy-start.1 = (f32[16,384,128]{2,0,1:T(8,128)S(1)}, f32[16,384,128]{2,0,1:T(8,128)}, u32[]{:S(2)}) copy-start(f32[16,384,128]{2,0,1:T(8,128)} %copy-done) | copy-start | bytes 9437188
  104.0 3.6 %collective-permute-start.2 = (f32[16,128]{1,0:T(8,128)S(1)}, f32[16,128]{1,0:T(8,128)S(1)}, u32[]{:S(2)}, u32[]{:S(2)}) collective-permute-start(f32[16,128]{1,0:T(8,128)S(1)} %get-tuple-element.32), channel_id=1, source_target_pairs={{0,8},{8,16},{16,24},{24,32},{32,40},{40,48},{48,56},{56,64},{64,7... | collective-permute-start | bytes 24584 | tf_op jit(solution)/shard_map/ppermute | solution.py:23
  106.3 4.4 %collective-permute-start.3 = (f32[16,128]{1,0:T(8,128)S(1)}, f32[16,128]{1,0:T(8,128)S(1)}, u32[]{:S(2)}, u32[]{:S(2)}) collective-permute-start(f32[16,128]{1,0:T(8,128)S(1)} %get-tuple-element.33), channel_id=1, source_target_pairs={{8,0},{16,8},{24,16},{32,24},{40,32},{48,40},{56,48},{64,56},{72,6... | collective-permute-start | bytes 24584 | tf_op jit(solution)/shard_map/ppermute | solution.py:25
  113.5 2.4 copy-start.9
  134.4 26.2 %all-to-all-start.2 = ((f32[128,1,1664]{2,1,0:T(1,128)}), f32[128,1,1664]{2,1,0:T(1,128)S(1)}, u32[]{:S(2)}, u32[]{:S(2)}) async-start(f32[128,1,1664]{2,1,0:T(1,128)} %copy.16), calls=%async_computation.2 | async-start | bytes 1703936 | tf_op jit(solution)/shard_map/all_to_all | solution.py:51
  161.4 1.5 copy-start.6
  163.0 1.7 copy-start.8
  164.6 1.0 copy-start.3
  164.9 1.7 copy-start.16
  164.9 1.7 copy-start.18
  164.9 1.7 copy-start.20
  198.9 9.7 %copy-start.2 = (f32[16,384,128]{2,0,1:T(8,128)S(1)}, f32[16,384,128]{2,0,1:T(8,128)}, u32[]{:S(2)}) copy-start(f32[16,384,128]{2,0,1:T(8,128)} %copy-done) | copy-start | bytes 9437188
  200.1 6.8 %copy-start.23 = (f32[16,4096]{1,0:T(8,128)}, f32[16,4096]{1,0:T(8,128)S(1)}, u32[]{:S(2)}) copy-start(f32[16,4096]{1,0:T(8,128)S(1)} %multiply_add_fusion) | copy-start | bytes 786436
  200.1 3.9 %collective-permute-start.4 = (f32[16,128]{1,0:T(8,128)S(1)}, f32[16,128]{1,0:T(8,128)S(1)}, u32[]{:S(2)}, u32[]{:S(2)}) collective-permute-start(f32[16,128]{1,0:T(8,128)S(1)} %get-tuple-element.30), channel_id=1, source_target_pairs={{0,8},{8,16},{16,24},{24,32},{32,40},{40,48},{48,56},{56,64},{64,7... | collective-permute-start | bytes 24584 | tf_op jit(solution)/shard_map/ppermute | solution.py:23
  202.4 4.4 %collective-permute-start.5 = (f32[16,128]{1,0:T(8,128)S(1)}, f32[16,128]{1,0:T(8,128)S(1)}, u32[]{:S(2)}, u32[]{:S(2)}) collective-permute-start(f32[16,128]{1,0:T(8,128)S(1)} %get-tuple-element.31), channel_id=1, source_target_pairs={{8,0},{16,8},{24,16},{32,24},{40,32},{48,40},{56,48},{64,56},{72,6... | collective-permute-start | bytes 24584 | tf_op jit(solution)/shard_map/ppermute | solution.py:25
  208.6 2.4 copy-start.24
  255.5 1.5 copy-start.4
  258.0 1.4 copy-start.11
  258.0 1.4 copy-start.13
  258.0 1.4 copy-start.15
  258.0 1.4 copy-start.17
  258.0 1.8 copy-start.19
  258.0 2.0 copy-start.21
